TPU v7x, 256 devices: a whole 4x4x8 slice. The times are simulated.
256 devices in a mesh: slab: 32 (over z, x), coil: 8 (over y, core).
Axes of the slice: x: 4, y: 4, z: 8, core: 2. Of those that a mesh axis runs over, the one named last changes fastest.
Arguments:
- noisy: float32 [2, 64, 256, 128], P(None, 'slab', 'coil'), may hold values from -6 to 6
- step_index: int32 [], replicated, may hold values from 200 to 599
- w_in: bfloat16 [3, 3, 3, 32, 2], replicated, may hold values from -0.875 to 0.875
- w_mid: bfloat16 [3, 3, 3, 32, 32], replicated, may hold values from -0.21875 to 0.21875
- w_out: bfloat16 [3, 3, 3, 2, 32], replicated, may hold values from -0.21875 to 0.21875
- time_weight: float32 [32, 32], replicated, may hold values from -1 to 1
- sens: float32 [16, 2, 64, 256, 128], P('coil', None, 'slab')
- kdata: float32 [16, 2, 64, 256, 128], P('coil', None, None, 'slab'), may hold values from -4 to 4
- mask: int32 [64, 256], P(None, 'slab'), may hold values from 0 to 1, as said below
Outputs:
- recon: float32 [2, 64, 256, 128], P(None, 'slab', 'coil')
- next_sample: float32 [2, 64, 256, 128], P(None, 'slab', 'coil')
Inputs may be any that keep to these rules, and one draw needn't show every extreme that they name: mask[kz, ky] is 1 wherever min(kz, 64 - kz) < max(1, 4) and min(ky, 256 - ky) < max(1, 8); every other entry is 1 with chance one in three.
All inputs are finite; a program needn't handle non-finite values.
Results may differ from a plain program's by a relative error of at most 0.0023.
Values may be sent and summed in bfloat16 or wider, within the bound.
No kernel may reach another device: no remote copies, remote signals or barrier semaphores. Data moves between devices by JAX's collectives and lax.ppermute only.
A program may use at most 64 MiB of HBM per device.

v0:
```python
import math

import jax
import jax.numpy as jnp
from jax import lax
from jax.sharding import PartitionSpec as P

ITERS = 2
STEPS = 1000
STRIDE = 20


REG_WEIGHT = 0.5
HIGHEST_PRECISION = lax.Precision.HIGHEST
TRANSFORM_PRECISION = lax.Precision.HIGH


def extended(cells, sides, width):
    for axis, dim in sides:
        count = lax.axis_size(axis)
        ends = count - 1
        head = lax.slice_in_dim(cells, 0, width, axis=dim)
        tail = lax.slice_in_dim(cells, cells.shape[dim] - width, cells.shape[dim], axis=dim)
        cells = jnp.concatenate(
            [
                lax.ppermute(tail, axis, [(i, (i + 1) % count) for i in range(ends)]),
                cells,
                lax.ppermute(head, axis, [((i + 1) % count, i) for i in range(ends)]),
            ],
            axis=dim,
        )
    return cells


def plan_level(step_value):
    angle = (step_value / STEPS + 0.008) / 1.008 * (math.pi / 2)
    return jnp.cos(angle) ** 2


def time_bias(step_value, time_weight):
    half = time_weight.shape[0] // 2
    freqs = jnp.exp(-math.log(10000.0) * jnp.arange(half, dtype=jnp.float32) / half)
    phase = step_value * freqs
    embed = jnp.concatenate([jnp.sin(phase), jnp.cos(phase)])
    return jnp.dot(embed, time_weight, precision=HIGHEST_PRECISION)


def conv_padded(padded, weights):
    depth, rows, width = (padded.shape[1] - 2, padded.shape[2] - 2, padded.shape[3])
    total = jnp.zeros((weights.shape[3], depth, rows, width), jnp.float32)
    for depth_shift in range(3):
        for row_shift in range(3):
            window = padded[:, depth_shift : depth_shift + depth, row_shift : row_shift + rows, :]
            taps = jnp.einsum(
                "aoc,czyx->aozyx",
                weights[depth_shift, row_shift],
                window,
                preferred_element_type=jnp.float32,
            )
            shifted = jnp.pad(taps, ((0, 0), (0, 0), (0, 0), (0, 0), (1, 1)))
            total = (
                total
                + shifted[0, ..., 0:width]
                + shifted[1, ..., 1 : width + 1]
                + shifted[2, ..., 2 : width + 2]
            )
    return total


def conv_layer(inputs, weights):
    return conv_padded(extended(inputs, (("slab", 1), ("coil", 2)), 1), weights)


def conv_shifted(padded, weights):
    depth, rows, width = (padded.shape[1] - 2, padded.shape[2] - 2, padded.shape[3])
    wide = jnp.pad(padded, ((0, 0), (0, 0), (0, 0), (1, 1)))
    stacked = jnp.concatenate([wide[..., c : c + width] for c in range(3)], axis=0)
    total = jnp.zeros((weights.shape[3], depth, rows, width), jnp.float32)
    for depth_shift in range(3):
        for row_shift in range(3):
            window = stacked[:, depth_shift : depth_shift + depth, row_shift : row_shift + rows, :]
            matrix = jnp.transpose(weights[depth_shift, row_shift], (1, 0, 2))
            matrix = matrix.reshape((weights.shape[3], -1))
            total = total + jnp.einsum(
                "ok,kzyx->ozyx", matrix, window, preferred_element_type=jnp.float32
            )
    return total


def conv_columns(padded, weights):
    depth, rows, width = (padded.shape[1] - 2, padded.shape[2] - 2, padded.shape[3])
    wide = jnp.pad(padded, ((0, 0), (0, 0), (0, 0), (1, 1)))
    windows = [
        wide[:, a : a + depth, b : b + rows, c : c + width]
        for a in range(3)
        for b in range(3)
        for c in range(3)
    ]
    columns = jnp.stack(windows, axis=0).reshape((-1, depth, rows, width))
    matrix = jnp.transpose(weights, (3, 0, 1, 2, 4)).reshape((weights.shape[3], -1))
    return jnp.einsum("ok,kzyx->ozyx", matrix, columns, preferred_element_type=jnp.float32)


def inside_volume(depth, rows):
    slab, slabs = lax.axis_index("slab"), lax.axis_size("slab")
    coil, coils = lax.axis_index("coil"), lax.axis_size("coil")
    plane = jnp.arange(depth)
    row = jnp.arange(rows)
    plane_ok = ~(((plane == 0) & (slab == 0)) | ((plane == depth - 1) & (slab == slabs - 1)))
    row_ok = ~(((row == 0) & (coil == 0)) | ((row == rows - 1) & (coil == coils - 1)))
    return plane_ok[:, None, None] & row_ok[None, :, None]


def dft_blocks(length, inverse):
    index = jnp.arange(length, dtype=jnp.int32)
    product = index[:, None] * index[None, :] % length
    theta = product.astype(jnp.float32) * (2.0 * math.pi / length)
    cosine = jnp.cos(theta) / math.sqrt(length)
    sine = jnp.sin(theta) / math.sqrt(length)
    if inverse:
        sine = -sine
    upper = jnp.stack([cosine, sine], axis=1)
    lower = jnp.stack([-sine, cosine], axis=1)
    return jnp.stack([upper, lower], axis=0)


def along_last(data, blocks):
    return jnp.einsum("pkqn,cqzyn->cpzyk", blocks, data, precision=TRANSFORM_PRECISION)


def along_rows(data, blocks):
    return jnp.einsum("pkqn,cqzny->cpzky", blocks, data, precision=TRANSFORM_PRECISION)


def along_depth(data, blocks):
    return jnp.einsum("pkqn,cqnyx->cpkyx", blocks, data, precision=TRANSFORM_PRECISION)


def times_sens(sens, image):
    real_part = sens[:, 0] * image[0] - sens[:, 1] * image[1]
    imag_part = sens[:, 0] * image[1] + sens[:, 1] * image[0]
    return jnp.stack([real_part, imag_part], axis=1)


def times_conj(sens, images):
    real_part = jnp.sum(sens[:, 0] * images[:, 0] + sens[:, 1] * images[:, 1], axis=0)
    imag_part = jnp.sum(sens[:, 0] * images[:, 1] - sens[:, 1] * images[:, 0], axis=0)
    return jnp.stack([real_part, imag_part])


def coil_term(image_full, sens, kdata_x, weight, blocks, with_data):
    forward_y, forward_z, inverse_y, inverse_z = blocks
    coil_images = times_sens(sens, image_full)
    spectrum = along_rows(coil_images, forward_y)
    pencils = lax.all_to_all(
        spectrum.astype(jnp.bfloat16), "slab", split_axis=3, concat_axis=2, tiled=True
    ).astype(jnp.float32)
    kspace = along_depth(pencils, forward_z)
    if with_data:
        kspace = weight * (kdata_x - kspace)
    else:
        kspace = weight * kspace
    back = along_depth(kspace, inverse_z)
    link_type = jnp.float32 if with_data else jnp.bfloat16
    slabs = lax.all_to_all(
        back.astype(link_type), "slab", split_axis=2, concat_axis=3, tiled=True
    ).astype(jnp.float32)
    images = along_rows(slabs, inverse_y)
    return times_conj(sens, images)


def combine_coils(partial_value):
    count = lax.axis_size("coil")
    pieces = lax.all_to_all(partial_value, "coil", split_axis=2, concat_axis=0, tiled=True)
    pieces = pieces.reshape((count, partial_value.shape[0]) + pieces.shape[1:])
    return jnp.sum(pieces, axis=0)


def gather_rows(value):
    return lax.all_gather(value, "coil", axis=2, tiled=True)


def global_sums(values):
    axes = ("slab", "coil")
    count = lax.axis_size("slab") * lax.axis_size("coil")
    spread = jnp.broadcast_to(values[None], (count,) + values.shape)
    return jnp.sum(lax.all_to_all(spread, axes, split_axis=0, concat_axis=0, tiled=True), axis=0)


def body(noisy, step_index, w_in, w_mid, w_out, time_weight, sens, kdata, mask):
    step_value = step_index.astype(jnp.float32)
    signal_level = plan_level(step_value)
    prior_level = plan_level(step_value - STRIDE)
    bias = time_bias(step_value, time_weight)
    noisy_wide = extended(noisy.astype(jnp.bfloat16), (("slab", 1), ("coil", 2)), 2)
    hidden_wide = jax.nn.silu(conv_columns(noisy_wide, w_in) + bias[:, None, None, None])
    hidden_wide = jnp.where(
        inside_volume(hidden_wide.shape[1], hidden_wide.shape[2]), hidden_wide, 0.0
    ).astype(jnp.bfloat16)
    hidden = hidden_wide[:, 1:-1, 1:-1, :]
    mixed = (hidden.astype(jnp.float32) + jax.nn.silu(conv_shifted(hidden_wide, w_mid))).astype(
        jnp.bfloat16
    )
    noise_pred = conv_layer(mixed, w_out)
    estimate = (noisy - jnp.sqrt(1.0 - signal_level) * noise_pred) / jnp.sqrt(signal_level)
    depth_full = kdata.shape[2]
    rows_full = sens.shape[3]
    width = sens.shape[4]
    blocks = (
        dft_blocks(rows_full, False),
        dft_blocks(depth_full, False),
        dft_blocks(rows_full, True),
        dft_blocks(depth_full, True),
    )
    kdata_x = along_last(kdata, dft_blocks(width, True))
    weight = mask.astype(jnp.float32)[None, None, :, :, None]

    def operator(image, with_data):
        return combine_coils(
            coil_term(gather_rows(image), sens, kdata_x, weight, blocks, with_data)
        )

    residual = operator(estimate, True)
    zero = jnp.zeros_like(residual)
    unknown = jnp.full((), jnp.inf, jnp.float32)

    def turn(_, state):
        solution, residual, direction, image, curvature, norm_now = state
        residual_image = operator(residual, False) + REG_WEIGHT * residual
        sums = global_sums(
            jnp.stack(
                [
                    jnp.sum(residual * residual),
                    jnp.sum(residual * residual_image),
                    jnp.sum(residual * image),
                    jnp.sum(direction * residual_image),
                ]
            )
        )
        norm_next = sums[0]
        ratio = norm_next / norm_now
        curvature = sums[1] + ratio * (sums[2] + sums[3]) + ratio * ratio * curvature
        direction = residual + ratio * direction
        image = residual_image + ratio * image
        step_size = norm_next / curvature
        solution = solution + step_size * direction
        residual = residual - step_size * image
        return (solution, residual, direction, image, curvature, norm_next)

    state = (estimate, residual, zero, zero, jnp.zeros((), jnp.float32), unknown)
    solution = lax.fori_loop(0, ITERS, turn, state)[0]
    recon = solution
    next_sample = jnp.sqrt(prior_level) * recon + jnp.sqrt(1.0 - prior_level) * noise_pred
    return (recon, next_sample)


def solution(mesh):
    return jax.shard_map(
        body,
        mesh=mesh,
        in_specs=(
            P(None, "slab", "coil", None),
            P(),
            P(),
            P(),
            P(),
            P(),
            P("coil", None, "slab", None, None),
            P("coil", None, None, "slab", None),
            P(None, "slab"),
        ),
        out_specs=(P(None, "slab", "coil", None), P(None, "slab", "coil", None)),
        check_vma=False,
    )
```

profile of v0, /device:TPU:1, one launch (start us, length us, event | category | flops | bytes accessed | tf_op | source)
XLA Modules:
  0.0 391.9 jit_solution(3931736955238933040)
XLA Ops:
  1.6 3.9 %collective-permute-start = (bf16[2,2,32,128]{3,2,1,0:T(8,128)(2,1)S(1)}, bf16[2,2,32,128]{3,2,1,0:T(8,128)(2,1)S(1)}, u32[]{:S(2)}, u32[]{:S(2)}) collective-permute-start(bf16[2,2,32,128]{3,2,1,0:T(8,128)(2,1)S(1)} %convert_element_type.146), channel_id=1, source_target_pairs={{0,8},{8,16},{16,24},{24,32},{32,40},{40,48},{48,56},{56,64},{64,7... | collective-permute-start | bytes 98312 | tf_op jit(solution)/shard_map/ppermute | solution.py:26
  5.5 1.3 collective-permute-start.1
  12.3 1.3 fusion.85
  13.7 4.0 %collective-permute-start.2 = (bf16[2,6,2,128]{3,2,1,0:T(2,128)(2,1)S(1)}, bf16[2,6,2,128]{3,2,1,0:T(2,128)(2,1)S(1)}, u32[]{:S(2)}, u32[]{:S(2)}) collective-permute-start(bf16[2,6,2,128]{3,2,1,0:T(2,128)(2,1)S(1)} %get-tuple-element.351), channel_id=1, source_target_pairs={{0,1},{1,2},{2,3},{3,4},{4,5},{5,6},{6,7},{8,9},{9,10},{10,11},{11... | collective-permute-start | bytes 18440 | tf_op jit(solution)/shard_map/ppermute | solution.py:26
  17.7 1.9 collective-permute-start.3
  20.9 1.8 collective-permute-done.3
  25.1 1.3 fusion.19
  31.6 4.3 %collective-permute-start.4 = (bf16[32,1,32,128]{3,0,2,1:T(8,128)(2,1)}, bf16[32,1,32,128]{3,0,2,1:T(8,128)(2,1)S(1)}, u32[]{:S(2)}, u32[]{:S(2)}) collective-permute-start(bf16[32,1,32,128]{3,0,2,1:T(8,128)(2,1)} %get-tuple-element.334), channel_id=1, source_target_pairs={{0,8},{8,16},{16,24},{24,32},{32,40},{40,48},{48,56},{56,64},{64,7... | collective-permute-start | bytes 786440 | tf_op jit(solution)/shard_map/ppermute | solution.py:26
  35.9 1.3 collective-permute-start.5
  38.1 1.6 copy.306
  40.9 4.1 %collective-permute-done.5 = bf16[32,1,32,128]{3,0,2,1:T(8,128)(2,1)} collective-permute-done((bf16[32,1,32,128]{3,0,2,1:T(8,128)(2,1)}, bf16[32,1,32,128]{3,0,2,1:T(8,128)(2,1)}, u32[]{:S(2)}, u32[]{:S(2)}) %collective-permute-start.5) | collective-permute-done | bytes 262176 | tf_op jit(solution)/shard_map/ppermute | solution.py:28
  45.7 4.1 %collective-permute-start.6 = (bf16[32,4,1,128]{3,0,2,1:T(8,128)(2,1)S(1)}, bf16[32,4,1,128]{3,0,2,1:T(8,128)(2,1)S(1)}, u32[]{:S(2)}, u32[]{:S(2)}) collective-permute-start(bf16[32,4,1,128]{3,0,2,1:T(8,128)(2,1)S(1)} %get-tuple-element.326), channel_id=1, source_target_pairs={{0,1},{1,2},{2,3},{3,4},{4,5},{5,6},{6,7},{8,9},{9,10},{10,11},{11... | collective-permute-start | bytes 98312 | tf_op jit(solution)/shard_map/ppermute | solution.py:26
  49.8 2.1 collective-permute-start.7
  53.4 1.7 collective-permute-done.7
  57.8 1.4 fusion.194
  60.5 12.8 %all_gather.6 = f32[2,2,256,128]{3,0,2,1:T(2,128)S(1)} all-gather(f32[2,2,32,128]{3,0,2,1:T(2,128)S(1)} %get-tuple-element.308), channel_id=1, replica_groups=mesh['slab'=32,'coil'=8] {'coil'}, dimensions={2}, use_global_device_ids=true | all-gather | bytes 589824 | tf_op jit(solution)/shard_map/all_gather | solution.py:180
  75.6 1.8 copy.310
  78.5 1.8 fusion.73
  80.3 2.0 copy.311
  82.3 16.6 %all-to-all-start.4 = ((bf16[2,2,2,256,128]{4,1,2,0,3:T(2,128)(2,1)}), bf16[2,2,2,256,128]{4,1,2,0,3:T(2,128)(2,1)}, u32[]{:S(2)}, u32[]{:S(2)}) async-start(bf16[2,2,2,256,128]{4,1,2,0,3:T(2,128)(2,1)} %copy.311), calls=%async_computation.4 | async-start | bytes 1048576 | tf_op jit(solution)/shard_map/all_to_all | solution.py:155
  100.7 1.7 convolution_bitcast_fusion.8
  102.4 13.2 %all-to-all-done.4 = bf16[2,2,2,256,128]{4,1,2,0,3:T(2,128)(2,1)} async-done(((bf16[2,2,2,256,128]{4,1,2,0,3:T(2,128)(2,1)}), bf16[2,2,2,256,128]{4,1,2,0,3:T(2,128)(2,1)}, u32[]{:S(2)}, u32[]{:S(2)}) %all-to-all-start.4) | async-done | bytes 524320 | tf_op jit(solution)/shard_map/all_to_all | solution.py:155
  119.0 30.7 %all_to_all.110 = f32[2,2,64,8,128]{4,1,3,0,2:T(2,128)S(1)} all-to-all(f32[2,2,64,8,128]{4,1,3,0,2:T(2,128)S(1)} %copy.315), channel_id=1, replica_groups=mesh['slab'=32,'coil'=8] {'slab'}, dimensions={2} | all-to-all | bytes 2097152 | tf_op jit(solution)/shard_map/all_to_all | solution.py:165
  149.8 1.9 convolution_bitcast_fusion.4
  152.7 2.0 copy.319
  154.7 7.3 %all-to-all-start.6 = ((f32[2,2,256,128]{3,1,0,2:T(2,128)}), f32[2,2,256,128]{3,1,0,2:T(2,128)}, u32[]{:S(2)}, u32[]{:S(2)}) async-start(f32[2,2,256,128]{3,1,0,2:T(2,128)} %copy.319), calls=%async_computation.6 | async-start | bytes 1048576 | tf_op jit(solution)/shard_map/all_to_all | solution.py:174
  162.2 1.6 pad_maximum_fusion.13
  163.8 2.8 pad_maximum_fusion.4
  166.6 4.9 %all-to-all-done.6 = f32[2,2,256,128]{3,1,0,2:T(2,128)} async-done(((f32[2,2,256,128]{3,1,0,2:T(2,128)}), f32[2,2,256,128]{3,1,0,2:T(2,128)}, u32[]{:S(2)}, u32[]{:S(2)}) %all-to-all-start.6) | async-done | bytes 524320 | tf_op jit(solution)/shard_map/all_to_all | solution.py:174
  173.4 216.3 %while.21 = (s32[]{:T(128)}, f32[2,2,32,128]{3,1,0,2:T(2,128)S(1)}, f32[2,2,32,128]{3,1,0,2:T(2,128)S(1)}, f32[2,2,32,128]{3,1,0,2:T(2,128)S(1)}, f32[2,2,32,128...) while((s32[]{:T(128)}, f32[2,2,32,128]{3,1,0,2:T(2,128)S(1)}, ...), condition=%wide.region_12.13_spmd.clone, body=%wide.region_3.12_spmd.clone.sunk | while | flops 2016658432 | bytes 33634820 | solution.py:251
  173.4 13.9 %all_gather.9 = f32[2,2,256,128]{3,1,0,2:T(2,128)S(1)} all-gather(f32[2,2,32,128]{3,1,0,2:T(2,128)S(1)} %get-tuple-element.524), channel_id=1, replica_groups=mesh['slab'=32,'coil'=8] {'coil'}, dimensions={2}, use_global_device_ids=true | all-gather | bytes 589824 | tf_op jit(solution)/shard_map/while/body/eval_jaxpr/all_gather | solution.py:180
  187.9 2.2 fusion.252
  190.7 21.9 %all_to_all.111 = bf16[2,2,2,256,128]{4,1,2,0,3:T(2,128)(2,1)S(1)} all-to-all(bf16[2,2,2,256,128]{4,1,2,0,3:T(2,128)(2,1)S(1)} %copy.475), channel_id=1, replica_groups=mesh['slab'=32,'coil'=8] {'slab'}, dimensions={3} | all-to-all | bytes 1048576 | tf_op jit(solution)/shard_map/while/body/eval_jaxpr/all_to_all | solution.py:155
  214.5 20.3 %all_to_all.112 = bf16[2,2,64,8,128]{4,1,3,0,2:T(2,128)(2,1)S(1)} all-to-all(bf16[2,2,64,8,128]{4,1,3,0,2:T(2,128)(2,1)S(1)} %copy.478), channel_id=1, replica_groups=mesh['slab'=32,'coil'=8] {'slab'}, dimensions={2} | all-to-all | bytes 1048576 | tf_op jit(solution)/shard_map/while/body/eval_jaxpr/all_to_all | solution.py:165
  237.0 6.7 %all-to-all-start.2 = ((f32[2,2,256,128]{3,1,0,2:T(2,128)}), f32[2,2,256,128]{3,1,0,2:T(2,128)S(1)}, u32[]{:S(2)}, u32[]{:S(2)}) async-start(f32[2,2,256,128]{3,1,0,2:T(2,128)} %copy.480), calls=%async_computation.2 | async-start | bytes 1048576 | tf_op jit(solution)/shard_map/while/body/eval_jaxpr/all_to_all | solution.py:174
  243.8 9.4 %all-to-all-done.2 = f32[2,2,256,128]{3,1,0,2:T(2,128)S(1)} async-done(((f32[2,2,256,128]{3,1,0,2:T(2,128)}), f32[2,2,256,128]{3,1,0,2:T(2,128)S(1)}, u32[]{:S(2)}, u32[]{:S(2)}) %all-to-all-start.2) | async-done | bytes 524320 | tf_op jit(solution)/shard_map/while/body/eval_jaxpr/all_to_all | solution.py:174
  254.2 2.7 pad_maximum_fusion.34
  257.6 6.3 %all-to-all-start.3 = ((f32[256,1,4]{2,1,0:T(1,128)}), f32[256,1,4]{2,1,0:T(1,128)S(1)}, u32[]{:S(2)}, u32[]{:S(2)}) async-start(f32[256,1,4]{2,1,0:T(1,128)} %broadcast_in_dim.26), calls=%async_computation.3 | async-start | bytes 262144 | tf_op jit(solution)/shard_map/while/body/eval_jaxpr/all_to_all | solution.py:187
  264.0 13.0 %all-to-all-done.3 = f32[256,1,4]{2,1,0:T(1,128)S(1)} async-done(((f32[256,1,4]{2,1,0:T(1,128)}), f32[256,1,4]{2,1,0:T(1,128)S(1)}, u32[]{:S(2)}, u32[]{:S(2)}) %all-to-all-start.3) | async-done | bytes 4128 | tf_op jit(solution)/shard_map/while/body/eval_jaxpr/all_to_all | solution.py:187
  282.7 13.4 %all_gather.9 = f32[2,2,256,128]{3,1,0,2:T(2,128)S(1)} all-gather(f32[2,2,32,128]{3,1,0,2:T(2,128)S(1)} %get-tuple-element.524), channel_id=1, replica_groups=mesh['slab'=32,'coil'=8] {'coil'}, dimensions={2}, use_global_device_ids=true | all-gather | bytes 589824 | tf_op jit(solution)/shard_map/while/body/eval_jaxpr/all_gather | solution.py:180
  296.7 2.2 fusion.252
  299.5 20.2 %all_to_all.111 = bf16[2,2,2,256,128]{4,1,2,0,3:T(2,128)(2,1)S(1)} all-to-all(bf16[2,2,2,256,128]{4,1,2,0,3:T(2,128)(2,1)S(1)} %copy.475), channel_id=1, replica_groups=mesh['slab'=32,'coil'=8] {'slab'}, dimensions={3} | all-to-all | bytes 1048576 | tf_op jit(solution)/shard_map/while/body/eval_jaxpr/all_to_all | solution.py:155
  321.5 20.3 %all_to_all.112 = bf16[2,2,64,8,128]{4,1,3,0,2:T(2,128)(2,1)S(1)} all-to-all(bf16[2,2,64,8,128]{4,1,3,0,2:T(2,128)(2,1)S(1)} %copy.478), channel_id=1, replica_groups=mesh['slab'=32,'coil'=8] {'slab'}, dimensions={2} | all-to-all | bytes 1048576 | tf_op jit(solution)/shard_map/while/body/eval_jaxpr/all_to_all | solution.py:165
  344.1 6.7 %all-to-all-start.2 = ((f32[2,2,256,128]{3,1,0,2:T(2,128)}), f32[2,2,256,128]{3,1,0,2:T(2,128)S(1)}, u32[]{:S(2)}, u32[]{:S(2)}) async-start(f32[2,2,256,128]{3,1,0,2:T(2,128)} %copy.480), calls=%async_computation.2 | async-start | bytes 1048576 | tf_op jit(solution)/shard_map/while/body/eval_jaxpr/all_to_all | solution.py:174
  350.8 9.4 %all-to-all-done.2 = f32[2,2,256,128]{3,1,0,2:T(2,128)S(1)} async-done(((f32[2,2,256,128]{3,1,0,2:T(2,128)}), f32[2,2,256,128]{3,1,0,2:T(2,128)S(1)}, u32[]{:S(2)}, u32[]{:S(2)}) %all-to-all-start.2) | async-done | bytes 524320 | tf_op jit(solution)/shard_map/while/body/eval_jaxpr/all_to_all | solution.py:174
  361.2 2.7 pad_maximum_fusion.34
  364.7 6.3 %all-to-all-start.3 = ((f32[256,1,4]{2,1,0:T(1,128)}), f32[256,1,4]{2,1,0:T(1,128)S(1)}, u32[]{:S(2)}, u32[]{:S(2)}) async-start(f32[256,1,4]{2,1,0:T(1,128)} %broadcast_in_dim.26), calls=%async_computation.3 | async-start | bytes 262144 | tf_op jit(solution)/shard_map/while/body/eval_jaxpr/all_to_all | solution.py:187
  371.0 13.0 %all-to-all-done.3 = f32[256,1,4]{2,1,0:T(1,128)S(1)} async-done(((f32[256,1,4]{2,1,0:T(1,128)}), f32[256,1,4]{2,1,0:T(1,128)S(1)}, u32[]{:S(2)}, u32[]{:S(2)}) %all-to-all-start.3) | async-done | bytes 4128 | tf_op jit(solution)/shard_map/while/body/eval_jaxpr/all_to_all | solution.py:187
  (195 shorter events, 53.2 us)
Async XLA Ops:
  0.6 100.1 %copy-start = (f32[2,2,64,8,128]{4,3,2,1,0:T(8,128)S(1)}, f32[2,2,64,8,128]{4,3,2,1,0:T(8,128)}, u32[]{:S(2)}) copy-start(f32[2,2,64,8,128]{4,3,2,1,0:T(8,128)} %param.18) | copy-start | bytes 3145732
  0.6 19.0 %copy-start.12 = (f32[32,32]{1,0:T(8,128)S(1)}, f32[32,32]{1,0:T(8,128)}, u32[]{:S(2)}) copy-start(f32[32,32]{1,0:T(8,128)} %param.16) | copy-start | bytes 12292
  0.7 19.2 %copy-start.13 = (bf16[3,3,3,32,2]{3,4,2,1,0:T(2,128)(2,1)S(1)}, bf16[3,3,3,32,2]{3,4,2,1,0:T(2,128)(2,1)}, u32[]{:S(2)}) copy-start(bf16[3,3,3,32,2]{3,4,2,1,0:T(2,128)(2,1)} %param.13) | copy-start | bytes 10372
  1.6 12.0 %collective-permute-start = (bf16[2,2,32,128]{3,2,1,0:T(8,128)(2,1)S(1)}, bf16[2,2,32,128]{3,2,1,0:T(8,128)(2,1)S(1)}, u32[]{:S(2)}, u32[]{:S(2)}) collective-permute-start(bf16[2,2,32,128]{3,2,1,0:T(8,128)(2,1)S(1)} %convert_element_type.146), channel_id=1, source_target_pairs={{0,8},{8,16},{16,24},{24,32},{32,40},{40,48},{48,56},{56,64},{64,7... | collective-permute-start | bytes 98312 | tf_op jit(solution)/shard_map/ppermute | solution.py:26
  5.5 8.1 %collective-permute-start.1 = (bf16[2,2,32,128]{3,2,1,0:T(8,128)(2,1)S(1)}, bf16[2,2,32,128]{3,2,1,0:T(8,128)(2,1)S(1)}, u32[]{:S(2)}, u32[]{:S(2)}) collective-permute-start(bf16[2,2,32,128]{3,2,1,0:T(8,128)(2,1)S(1)} %convert_element_type.146), channel_id=1, source_target_pairs={{8,0},{16,8},{24,16},{32,24},{40,32},{48,40},{56,48},{64,56},{72,6... | collective-permute-start | bytes 98312 | tf_op jit(solution)/shard_map/ppermute | solution.py:28
  13.7 7.2 %collective-permute-start.2 = (bf16[2,6,2,128]{3,2,1,0:T(2,128)(2,1)S(1)}, bf16[2,6,2,128]{3,2,1,0:T(2,128)(2,1)S(1)}, u32[]{:S(2)}, u32[]{:S(2)}) collective-permute-start(bf16[2,6,2,128]{3,2,1,0:T(2,128)(2,1)S(1)} %get-tuple-element.351), channel_id=1, source_target_pairs={{0,1},{1,2},{2,3},{3,4},{4,5},{5,6},{6,7},{8,9},{9,10},{10,11},{11... | collective-permute-start | bytes 18440 | tf_op jit(solution)/shard_map/ppermute | solution.py:26
  17.7 4.9 %collective-permute-start.3 = (bf16[2,6,2,128]{3,2,1,0:T(2,128)(2,1)S(1)}, bf16[2,6,2,128]{3,2,1,0:T(2,128)(2,1)S(1)}, u32[]{:S(2)}, u32[]{:S(2)}) collective-permute-start(bf16[2,6,2,128]{3,2,1,0:T(2,128)(2,1)S(1)} %get-tuple-element.352), channel_id=1, source_target_pairs={{1,0},{2,1},{3,2},{4,3},{5,4},{6,5},{7,6},{9,8},{10,9},{11,10},{12... | collective-permute-start | bytes 18440 | tf_op jit(solution)/shard_map/ppermute | solution.py:28
  31.6 9.3 %collective-permute-start.4 = (bf16[32,1,32,128]{3,0,2,1:T(8,128)(2,1)}, bf16[32,1,32,128]{3,0,2,1:T(8,128)(2,1)S(1)}, u32[]{:S(2)}, u32[]{:S(2)}) collective-permute-start(bf16[32,1,32,128]{3,0,2,1:T(8,128)(2,1)} %get-tuple-element.334), channel_id=1, source_target_pairs={{0,8},{8,16},{16,24},{24,32},{32,40},{40,48},{48,56},{56,64},{64,7... | collective-permute-start | bytes 786440 | tf_op jit(solution)/shard_map/ppermute | solution.py:26
  35.9 9.1 %collective-permute-start.5 = (bf16[32,1,32,128]{3,0,2,1:T(8,128)(2,1)}, bf16[32,1,32,128]{3,0,2,1:T(8,128)(2,1)}, u32[]{:S(2)}, u32[]{:S(2)}) collective-permute-start(bf16[32,1,32,128]{3,0,2,1:T(8,128)(2,1)} %get-tuple-element.335), channel_id=1, source_target_pairs={{8,0},{16,8},{24,16},{32,24},{40,32},{48,40},{56,48},{64,56},{72,6... | collective-permute-start | bytes 786440 | tf_op jit(solution)/shard_map/ppermute | solution.py:28
  45.7 7.6 %collective-permute-start.6 = (bf16[32,4,1,128]{3,0,2,1:T(8,128)(2,1)S(1)}, bf16[32,4,1,128]{3,0,2,1:T(8,128)(2,1)S(1)}, u32[]{:S(2)}, u32[]{:S(2)}) collective-permute-start(bf16[32,4,1,128]{3,0,2,1:T(8,128)(2,1)S(1)} %get-tuple-element.326), channel_id=1, source_target_pairs={{0,1},{1,2},{2,3},{3,4},{4,5},{5,6},{6,7},{8,9},{9,10},{10,11},{11... | collective-permute-start | bytes 98312 | tf_op jit(solution)/shard_map/ppermute | solution.py:26
  49.8 5.2 %collective-permute-start.7 = (bf16[32,4,1,128]{3,0,2,1:T(8,128)(2,1)S(1)}, bf16[32,4,1,128]{3,0,2,1:T(8,128)(2,1)S(1)}, u32[]{:S(2)}, u32[]{:S(2)}) collective-permute-start(bf16[32,4,1,128]{3,0,2,1:T(8,128)(2,1)S(1)} %get-tuple-element.327), channel_id=1, source_target_pairs={{1,0},{2,1},{3,2},{4,3},{5,4},{6,5},{7,6},{9,8},{10,9},{11,10},{12... | collective-permute-start | bytes 98312 | tf_op jit(solution)/shard_map/ppermute | solution.py:28
  57.1 2.2 copy-start.11
  60.5 14.0 %copy-start.7 = (f32[2,2,32,128]{3,0,2,1:T(2,128)}, f32[2,2,32,128]{3,0,2,1:T(2,128)S(1)}, u32[]{:S(2)}) copy-start(f32[2,2,32,128]{3,0,2,1:T(2,128)S(1)} %get-tuple-element.308) | copy-start | bytes 196612
  73.3 5.2 %copy-start.2 = (f32[1,256,2,256]{3,1,2,0:T(8,128)S(1)}, f32[1,256,2,256]{3,1,2,0:T(8,128)}, u32[]{:S(2)}) copy-start(f32[1,256,2,256]{3,1,2,0:T(8,128)} %get-tuple-element.336) | copy-start | bytes 1572868
  82.3 20.1 %copy-start.14 = (s32[64,8]{0,1:T(8,128)S(1)}, s32[64,8]{0,1:T(8,128)}, u32[]{:S(2)}) copy-start(s32[64,8]{0,1:T(8,128)} %param.19) | copy-start | bytes 6148
  82.3 33.3 %all-to-all-start.4 = ((bf16[2,2,2,256,128]{4,1,2,0,3:T(2,128)(2,1)}), bf16[2,2,2,256,128]{4,1,2,0,3:T(2,128)(2,1)}, u32[]{:S(2)}, u32[]{:S(2)}) async-start(bf16[2,2,2,256,128]{4,1,2,0,3:T(2,128)(2,1)} %copy.311), calls=%async_computation.4 | async-start | bytes 1048576 | tf_op jit(solution)/shard_map/all_to_all | solution.py:155
  100.7 16.2 %copy-start.9 = (f32[1,64,2,64]{3,1,2,0:T(8,128)}, f32[1,64,2,64]{3,1,2,0:T(8,128)S(1)}, u32[]{:S(2)}) copy-start(f32[1,64,2,64]{3,1,2,0:T(8,128)S(1)} %get-tuple-element.359) | copy-start | bytes 98308
  100.7 16.8 %copy-start.10 = (f32[1,64,2,64]{3,1,2,0:T(8,128)}, f32[1,64,2,64]{3,1,2,0:T(8,128)S(1)}, u32[]{:S(2)}) copy-start(f32[1,64,2,64]{3,1,2,0:T(8,128)S(1)} %get-tuple-element.360) | copy-start | bytes 98308
  115.6 1.4 copy-start.6
  119.0 30.8 %copy-start.3 = (f32[1,256,2,256]{3,1,2,0:T(8,128)S(1)}, f32[1,256,2,256]{3,1,2,0:T(8,128)}, u32[]{:S(2)}) copy-start(f32[1,256,2,256]{3,1,2,0:T(8,128)} %get-tuple-element.328) | copy-start | bytes 1572868
  119.0 30.8 %copy-start.4 = (f32[1,256,2,256]{3,1,2,0:T(8,128)S(1)}, f32[1,256,2,256]{3,1,2,0:T(8,128)}, u32[]{:S(2)}) copy-start(f32[1,256,2,256]{3,1,2,0:T(8,128)} %get-tuple-element.337) | copy-start | bytes 1572868
  154.7 16.8 %all-to-all-start.6 = ((f32[2,2,256,128]{3,1,0,2:T(2,128)}), f32[2,2,256,128]{3,1,0,2:T(2,128)}, u32[]{:S(2)}, u32[]{:S(2)}) async-start(f32[2,2,256,128]{3,1,0,2:T(2,128)} %copy.319), calls=%async_computation.6 | async-start | bytes 1048576 | tf_op jit(solution)/shard_map/all_to_all | solution.py:174
  163.8 2.8 copy-start.8
  190.7 22.6 %copy-start.5 = (f32[2,64,2,64]{3,1,2,0:T(8,128)S(1)}, f32[2,64,2,64]{3,1,2,0:T(8,128)}, u32[]{:S(2)}) copy-start(f32[2,64,2,64]{3,1,2,0:T(8,128)} %get-tuple-element.550) | copy-start | bytes 196612 | tf_op jit(solution)/shard_map/while
  213.3 21.6 %copy-start.1 = (f32[2,256,2,256]{3,1,2,0:T(8,128)S(1)}, f32[2,256,2,256]{3,1,2,0:T(8,128)}, u32[]{:S(2)}) copy-start(f32[2,256,2,256]{3,1,2,0:T(8,128)} %get-tuple-element.551) | copy-start | bytes 3145732 | tf_op jit(solution)/shard_map/while
  237.0 16.1 %all-to-all-start.2 = ((f32[2,2,256,128]{3,1,0,2:T(2,128)}), f32[2,2,256,128]{3,1,0,2:T(2,128)S(1)}, u32[]{:S(2)}, u32[]{:S(2)}) async-start(f32[2,2,256,128]{3,1,0,2:T(2,128)} %copy.480), calls=%async_computation.2 | async-start | bytes 1048576 | tf_op jit(solution)/shard_map/while/body/eval_jaxpr/all_to_all | solution.py:174
  257.6 19.3 %all-to-all-start.3 = ((f32[256,1,4]{2,1,0:T(1,128)}), f32[256,1,4]{2,1,0:T(1,128)S(1)}, u32[]{:S(2)}, u32[]{:S(2)}) async-start(f32[256,1,4]{2,1,0:T(1,128)} %broadcast_in_dim.26), calls=%async_computation.3 | async-start | bytes 262144 | tf_op jit(solution)/shard_map/while/body/eval_jaxpr/all_to_all | solution.py:187
  299.5 20.8 %copy-start.5 = (f32[2,64,2,64]{3,1,2,0:T(8,128)S(1)}, f32[2,64,2,64]{3,1,2,0:T(8,128)}, u32[]{:S(2)}) copy-start(f32[2,64,2,64]{3,1,2,0:T(8,128)} %get-tuple-element.550) | copy-start | bytes 196612 | tf_op jit(solution)/shard_map/while
  320.3 21.6 %copy-start.1 = (f32[2,256,2,256]{3,1,2,0:T(8,128)S(1)}, f32[2,256,2,256]{3,1,2,0:T(8,128)}, u32[]{:S(2)}) copy-start(f32[2,256,2,256]{3,1,2,0:T(8,128)} %get-tuple-element.551) | copy-start | bytes 3145732 | tf_op jit(solution)/shard_map/while
  344.1 16.1 %all-to-all-start.2 = ((f32[2,2,256,128]{3,1,0,2:T(2,128)}), f32[2,2,256,128]{3,1,0,2:T(2,128)S(1)}, u32[]{:S(2)}, u32[]{:S(2)}) async-start(f32[2,2,256,128]{3,1,0,2:T(2,128)} %copy.480), calls=%async_computation.2 | async-start | bytes 1048576 | tf_op jit(solution)/shard_map/while/body/eval_jaxpr/all_to_all | solution.py:174
  364.7 19.3 %all-to-all-start.3 = ((f32[256,1,4]{2,1,0:T(1,128)}), f32[256,1,4]{2,1,0:T(1,128)S(1)}, u32[]{:S(2)}, u32[]{:S(2)}) async-start(f32[256,1,4]{2,1,0:T(1,128)} %broadcast_in_dim.26), calls=%async_computation.3 | async-start | bytes 262144 | tf_op jit(solution)/shard_map/while/body/eval_jaxpr/all_to_all | solution.py:187
where the time goes:
time: 394 us; the launch traced here: 392 us
  blocking collectives  154 us (39%)
  starting transfers between devices  73.1 us (19%)
  waiting for transfers between devices  71.5 us (18%)
  other arithmetic  32.2 us (8%)
  local copies, waits for them, and re-layouts  28.1 us (7%)
  matrix products  22.9 us (6%)
  loops' own time  8.35 us (2%)
    all_to_all x3, blocking collectives, coil_term(): lax.all_to_all(back.astype(link_type), 'slab', split_axis=2, concat_axis=...  71.3 us
    all_to_all x2, blocking collectives, coil_term(): lax.all_to_all(spectrum.astype(jnp.bfloat16), 'slab', split_axis=3, conca...  42.1 us
    all_gather x3, blocking collectives, gather_rows(): return lax.all_gather(value, 'coil', axis=2, tiled=True)  40.1 us
    all_to_all x2, waiting for transfers between devices, global_sums(): lax.all_to_all(spread, axes, split_axis=0, concat_axis=0, tiled=True)  26 us
    all_to_all x3, waiting for transfers between devices, combine_coils(): lax.all_to_all(partial_value, 'coil', split_axis=2, concat_axis=0, tiled=...  23.7 us
    all_to_all x3, starting transfers between devices, combine_coils(): lax.all_to_all(partial_value, 'coil', split_axis=2, concat_axis=0, tiled=...  20.8 us
    all_to_all x1, starting transfers between devices, coil_term(): lax.all_to_all(spectrum.astype(jnp.bfloat16), 'slab', split_axis=3, conca...  16.6 us
    ppermute x4, starting transfers between devices, extended(): lax.ppermute(tail, axis, [(i, (i + 1) % count) for i in range(ends)])  16.4 us
  transfers between devices with their start and end apart: 14, of which 10 were waited for; matrix products, arithmetic and copies ran while one was open for 5% of the time, Pallas kernels for 0%

commit v1 on v0

--- a/solution.py
+++ b/solution.py
@@ -47,10 +47,11 @@
 
 def conv_padded(padded, weights):
     depth, rows, width = (padded.shape[1] - 2, padded.shape[2] - 2, padded.shape[3])
-    total = jnp.zeros((weights.shape[3], depth, rows, width), jnp.float32)
-    for depth_shift in range(3):
+
+    def plane_taps(depth_shift, total):
+        planes = lax.dynamic_slice_in_dim(padded, depth_shift, depth, axis=1)
         for row_shift in range(3):
-            window = padded[:, depth_shift : depth_shift + depth, row_shift : row_shift + rows, :]
+            window = planes[:, :, row_shift : row_shift + rows, :]
             taps = jnp.einsum(
                 "aoc,czyx->aozyx",
                 weights[depth_shift, row_shift],
@@ -64,7 +65,10 @@
                 + shifted[1, ..., 1 : width + 1]
                 + shifted[2, ..., 2 : width + 2]
             )
-    return total
+        return total
+
+    total = jnp.zeros((weights.shape[3], depth, rows, width), jnp.float32)
+    return lax.fori_loop(0, 3, plane_taps, total)
 
 
 def conv_layer(inputs, weights):
@@ -75,16 +79,19 @@
     depth, rows, width = (padded.shape[1] - 2, padded.shape[2] - 2, padded.shape[3])
     wide = jnp.pad(padded, ((0, 0), (0, 0), (0, 0), (1, 1)))
     stacked = jnp.concatenate([wide[..., c : c + width] for c in range(3)], axis=0)
-    total = jnp.zeros((weights.shape[3], depth, rows, width), jnp.float32)
-    for depth_shift in range(3):
+    def plane_taps(depth_shift, total):
+        planes = lax.dynamic_slice_in_dim(stacked, depth_shift, depth, axis=1)
         for row_shift in range(3):
-            window = stacked[:, depth_shift : depth_shift + depth, row_shift : row_shift + rows, :]
+            window = planes[:, :, row_shift : row_shift + rows, :]
             matrix = jnp.transpose(weights[depth_shift, row_shift], (1, 0, 2))
             matrix = matrix.reshape((weights.shape[3], -1))
             total = total + jnp.einsum(
                 "ok,kzyx->ozyx", matrix, window, preferred_element_type=jnp.float32
             )
-    return total
+        return total
+
+    total = jnp.zeros((weights.shape[3], depth, rows, width), jnp.float32)
+    return lax.fori_loop(0, 3, plane_taps, total)
 
 
 def conv_columns(padded, weights):

time: 394 us -> 424 us (1.076)
  matrix products: 22.9 us -> 44.7 us
  other arithmetic: 32.2 us -> 38.7 us
    dot_general x18, matrix products: 6.36 us -> 27.5 us  [the longest x9 19.6 us: plane_taps(): jnp.einsum('ok,kzyx->ozyx', matrix, window, preferred_element_type=jnp.fl...]
  transfers between devices with their start and end apart: 14 -> 14, of which waited for: 10 -> 10; matrix products, arithmetic and copies ran while one was open for 5% -> 4% of each run, Pallas kernels for 0% -> 0%
where the time goes in v1:
time: 424 us; the launch traced here: 422 us
  blocking collectives  154 us (36%)
  starting transfers between devices  73.7 us (17%)
  waiting for transfers between devices  69.9 us (16%)
  matrix products  44.7 us (11%)
  other arithmetic  38.7 us (9%)
  local copies, waits for them, and re-layouts  30.7 us (7%)
  loops' own time  7.75 us (2%)
    all_to_all x3, blocking collectives, coil_term(): lax.all_to_all(back.astype(link_type), 'slab', split_axis=2, concat_axis=...  71.5 us
    all_to_all x2, blocking collectives, coil_term(): lax.all_to_all(spectrum.astype(jnp.bfloat16), 'slab', split_axis=3, conca...  42.1 us
    all_gather x3, blocking collectives, gather_rows(): return lax.all_gather(value, 'coil', axis=2, tiled=True)  40.4 us
    all_to_all x2, waiting for transfers between devices, global_sums(): lax.all_to_all(spread, axes, split_axis=0, concat_axis=0, tiled=True)  25.9 us
    all_to_all x3, waiting for transfers between devices, combine_coils(): lax.all_to_all(partial_value, 'coil', split_axis=2, concat_axis=0, tiled=...  23.7 us
    all_to_all x3, starting transfers between devices, combine_coils(): lax.all_to_all(partial_value, 'coil', split_axis=2, concat_axis=0, tiled=...  20.7 us
    dot_general x9, matrix products, plane_taps(): jnp.einsum('ok,kzyx->ozyx', matrix, window, preferred_element_type=jnp.fl...  19.6 us
    ppermute x4, starting transfers between devices, extended(): lax.ppermute(tail, axis, [(i, (i + 1) % count) for i in range(ends)])  17.3 us
  transfers between devices with their start and end apart: 14, of which 10 were waited for; matrix products, arithmetic and copies ran while one was open for 4% of the time, Pallas kernels for 0%

profile of v1, /device:TPU:1, one launch (start us, length us, event | category | flops | bytes accessed | tf_op | source)
XLA Modules:
  0.0 421.8 jit_solution(2014717687961791956)
XLA Ops:
  1.6 3.9 collective-permute-start
  11.1 4.3 %collective-permute-start.2 = (bf16[2,6,2,128]{3,2,1,0:T(2,128)(2,1)S(1)}, bf16[2,6,2,128]{3,2,1,0:T(2,128)(2,1)S(1)}, u32[]{:S(2)}, u32[]{:S(2)}) collective-permute-start(bf16[2,6,2,128]{3,2,1,0:T(2,128)(2,1)S(1)} %get-tuple-element.626), channel_id=1, source_target_pairs={{0,1},{1,2},{2,3},{3,4},{4,5},{5,6},{6,7},{8,9},{9,10},{10,11},{11... | collective-permute-start | bytes 18440 | tf_op jit(solution)/shard_map/ppermute | solution.py:26
  15.4 1.9 collective-permute-start.3
  24.8 1.8 pad_maximum_fusion.2
  26.6 20.6 %while.51 = (s32[]{:T(128)}, f32[32,2,32,128]{3,0,2,1:T(8,128)}, bf16[3,3,3,32,32]{4,2,3,1,0:T(4,128)(2,1)S(1)}, bf16[96,4,34,128]{3,0,2,1:T(8,128)(2,1)}, s32[]{:T(128)}, /*index=5*/s32[]{:T(128)}, s32[]{}, s32[]{}) while((s32[]{:T(128)}, f32[32,2,32,128]{3,0,2,1:T(8,128)}, bf16[3,3,3,32,32]{4,2,3,1,0:T(4,128)(2,1)S(1)}, ...), condition=%wide.region_1.2_spmd.clone, body=%wide.region_0.1_spmd.clone.sunk | while | flops 152043520 | bytes 11103875 | solution.py:94
  28.6 1.8 fusion.212
  30.4 2.8 fusion.213
  35.2 1.8 fusion.212
  37.1 3.1 fusion.213
  40.4 1.8 fusion.211
  42.2 1.8 fusion.212
  44.0 3.1 fusion.213
  49.0 4.1 collective-permute-start.4
  57.8 4.1 collective-permute-done.5
  62.6 4.9 %collective-permute-start.6 = (bf16[32,4,1,128]{3,0,2,1:T(8,128)(2,1)}, bf16[32,4,1,128]{3,0,2,1:T(8,128)(2,1)S(1)}, u32[]{:S(2)}, u32[]{:S(2)}) collective-permute-start(bf16[32,4,1,128]{3,0,2,1:T(8,128)(2,1)} %get-tuple-element.612), channel_id=1, source_target_pairs={{0,1},{1,2},{2,3},{3,4},{4,5},{5,6},{6,7},{8,9},{9,10},{10,11},{11... | collective-permute-start | bytes 98312 | tf_op jit(solution)/shard_map/ppermute | solution.py:26
  67.5 1.9 collective-permute-start.7
  74.2 15.8 %while.52 = (s32[]{:T(128)}, f32[2,2,32,128]{3,2,1,0:T(8,128)S(1)}, bf16[3,3,3,2,32]{4,2,3,1,0:T(4,128)(2,1)}, bf16[32,4,34,128]{3,0,2,1:T(8,128)(2,1)S(1)}, s32[]{:T(128)}, /*index=5*/s32[]{:T(128)}, s32[]{}, s32[]{}) while((s32[]{:T(128)}, f32[2,2,32,128]{3,2,1,0:T(8,128)S(1)}, bf16[3,3,3,2,32]{4,2,3,1,0:T(4,128)(2,1)}, ...), condition=%wide.region_3.4_spmd.clone, body=%wide.region_2.3_spmd.clone.sunk | while | flops 9601029 | bytes 4400255 | solution.py:71
  91.6 13.0 %all_gather.6 = f32[2,2,256,128]{3,1,0,2:T(2,128)S(1)} all-gather(f32[2,2,32,128]{3,1,0,2:T(2,128)S(1)} %fusion.153), channel_id=1, replica_groups=mesh['slab'=32,'coil'=8] {'coil'}, dimensions={2}, use_global_device_ids=true | all-gather | bytes 589824 | tf_op jit(solution)/shard_map/all_gather | solution.py:187
  106.7 1.8 copy.200
  109.6 1.8 fusion.78
  111.5 2.0 copy.201
  113.5 16.7 %all-to-all-start.4 = ((bf16[2,2,2,256,128]{4,1,2,0,3:T(2,128)(2,1)}), bf16[2,2,2,256,128]{4,1,2,0,3:T(2,128)(2,1)}, u32[]{:S(2)}, u32[]{:S(2)}) async-start(bf16[2,2,2,256,128]{4,1,2,0,3:T(2,128)(2,1)} %copy.201), calls=%async_computation.4 | async-start | bytes 1048576 | tf_op jit(solution)/shard_map/all_to_all | solution.py:162
  132.8 14.0 %all-to-all-done.4 = bf16[2,2,2,256,128]{4,1,2,0,3:T(2,128)(2,1)} async-done(((bf16[2,2,2,256,128]{4,1,2,0,3:T(2,128)(2,1)}), bf16[2,2,2,256,128]{4,1,2,0,3:T(2,128)(2,1)}, u32[]{:S(2)}, u32[]{:S(2)}) %all-to-all-start.4) | async-done | bytes 524320 | tf_op jit(solution)/shard_map/all_to_all | solution.py:162
  150.2 30.8 %all_to_all.110 = f32[2,2,64,8,128]{4,1,3,0,2:T(2,128)S(1)} all-to-all(f32[2,2,64,8,128]{4,1,3,0,2:T(2,128)S(1)} %copy.205), channel_id=1, replica_groups=mesh['slab'=32,'coil'=8] {'slab'}, dimensions={2} | all-to-all | bytes 2097152 | tf_op jit(solution)/shard_map/all_to_all | solution.py:172
  181.1 1.9 convolution_bitcast_fusion.4
  184.1 2.1 copy.209
  186.1 7.2 %all-to-all-start.6 = ((f32[2,2,256,128]{3,1,0,2:T(2,128)}), f32[2,2,256,128]{3,1,0,2:T(2,128)}, u32[]{:S(2)}, u32[]{:S(2)}) async-start(f32[2,2,256,128]{3,1,0,2:T(2,128)} %copy.209), calls=%async_computation.6 | async-start | bytes 1048576 | tf_op jit(solution)/shard_map/all_to_all | solution.py:181
  195.1 2.7 pad_maximum_fusion.4
  197.8 5.0 %all-to-all-done.6 = f32[2,2,256,128]{3,1,0,2:T(2,128)} async-done(((f32[2,2,256,128]{3,1,0,2:T(2,128)}), f32[2,2,256,128]{3,1,0,2:T(2,128)}, u32[]{:S(2)}, u32[]{:S(2)}) %all-to-all-start.6) | async-done | bytes 524320 | tf_op jit(solution)/shard_map/all_to_all | solution.py:181
  204.7 215.6 %while.53 = (s32[]{:T(128)}, f32[2,2,32,128]{3,1,0,2:T(2,128)S(1)}, f32[2,2,32,128]{3,1,0,2:T(2,128)S(1)}, f32[2,2,32,128]{3,1,0,2:T(2,128)S(1)}, f32[2,2,32,128...) while((s32[]{:T(128)}, f32[2,2,32,128]{3,1,0,2:T(2,128)S(1)}, ...), condition=%wide.region_16.17_spmd.clone, body=%wide.region_7.16_spmd.clone.sunk | while | flops 2016658432 | bytes 33634820 | solution.py:258
  204.7 13.9 %all_gather.9 = f32[2,2,256,128]{3,1,0,2:T(2,128)S(1)} all-gather(f32[2,2,32,128]{3,1,0,2:T(2,128)S(1)} %get-tuple-element.890), channel_id=1, replica_groups=mesh['slab'=32,'coil'=8] {'coil'}, dimensions={2}, use_global_device_ids=true | all-gather | bytes 589824 | tf_op jit(solution)/shard_map/while/body/eval_jaxpr/all_gather | solution.py:187
  219.2 2.2 fusion.228
  222.0 21.9 %all_to_all.111 = bf16[2,2,2,256,128]{4,1,2,0,3:T(2,128)(2,1)S(1)} all-to-all(bf16[2,2,2,256,128]{4,1,2,0,3:T(2,128)(2,1)S(1)} %copy.318), channel_id=1, replica_groups=mesh['slab'=32,'coil'=8] {'slab'}, dimensions={3} | all-to-all | bytes 1048576 | tf_op jit(solution)/shard_map/while/body/eval_jaxpr/all_to_all | solution.py:162
  245.8 20.3 %all_to_all.112 = bf16[2,2,64,8,128]{4,1,3,0,2:T(2,128)(2,1)S(1)} all-to-all(bf16[2,2,64,8,128]{4,1,3,0,2:T(2,128)(2,1)S(1)} %copy.321), channel_id=1, replica_groups=mesh['slab'=32,'coil'=8] {'slab'}, dimensions={2} | all-to-all | bytes 1048576 | tf_op jit(solution)/shard_map/while/body/eval_jaxpr/all_to_all | solution.py:172
  268.3 6.7 %all-to-all-start.2 = ((f32[2,2,256,128]{3,1,0,2:T(2,128)}), f32[2,2,256,128]{3,1,0,2:T(2,128)S(1)}, u32[]{:S(2)}, u32[]{:S(2)}) async-start(f32[2,2,256,128]{3,1,0,2:T(2,128)} %copy.323), calls=%async_computation.2 | async-start | bytes 1048576 | tf_op jit(solution)/shard_map/while/body/eval_jaxpr/all_to_all | solution.py:181
  275.1 9.4 %all-to-all-done.2 = f32[2,2,256,128]{3,1,0,2:T(2,128)S(1)} async-done(((f32[2,2,256,128]{3,1,0,2:T(2,128)}), f32[2,2,256,128]{3,1,0,2:T(2,128)S(1)}, u32[]{:S(2)}, u32[]{:S(2)}) %all-to-all-start.2) | async-done | bytes 524320 | tf_op jit(solution)/shard_map/while/body/eval_jaxpr/all_to_all | solution.py:181
  285.5 2.7 pad_maximum_fusion.32
  288.9 6.3 %all-to-all-start.3 = ((f32[256,1,4]{2,1,0:T(1,128)}), f32[256,1,4]{2,1,0:T(1,128)S(1)}, u32[]{:S(2)}, u32[]{:S(2)}) async-start(f32[256,1,4]{2,1,0:T(1,128)} %broadcast_in_dim.26), calls=%async_computation.3 | async-start | bytes 262144 | tf_op jit(solution)/shard_map/while/body/eval_jaxpr/all_to_all | solution.py:194
  295.2 13.0 %all-to-all-done.3 = f32[256,1,4]{2,1,0:T(1,128)S(1)} async-done(((f32[256,1,4]{2,1,0:T(1,128)}), f32[256,1,4]{2,1,0:T(1,128)S(1)}, u32[]{:S(2)}, u32[]{:S(2)}) %all-to-all-start.3) | async-done | bytes 4128 | tf_op jit(solution)/shard_map/while/body/eval_jaxpr/all_to_all | solution.py:194
  313.6 13.5 %all_gather.9 = f32[2,2,256,128]{3,1,0,2:T(2,128)S(1)} all-gather(f32[2,2,32,128]{3,1,0,2:T(2,128)S(1)} %get-tuple-element.890), channel_id=1, replica_groups=mesh['slab'=32,'coil'=8] {'coil'}, dimensions={2}, use_global_device_ids=true | all-gather | bytes 589824 | tf_op jit(solution)/shard_map/while/body/eval_jaxpr/all_gather | solution.py:187
  327.7 2.2 fusion.228
  330.4 20.1 %all_to_all.111 = bf16[2,2,2,256,128]{4,1,2,0,3:T(2,128)(2,1)S(1)} all-to-all(bf16[2,2,2,256,128]{4,1,2,0,3:T(2,128)(2,1)S(1)} %copy.318), channel_id=1, replica_groups=mesh['slab'=32,'coil'=8] {'slab'}, dimensions={3} | all-to-all | bytes 1048576 | tf_op jit(solution)/shard_map/while/body/eval_jaxpr/all_to_all | solution.py:162
  352.4 20.3 %all_to_all.112 = bf16[2,2,64,8,128]{4,1,3,0,2:T(2,128)(2,1)S(1)} all-to-all(bf16[2,2,64,8,128]{4,1,3,0,2:T(2,128)(2,1)S(1)} %copy.321), channel_id=1, replica_groups=mesh['slab'=32,'coil'=8] {'slab'}, dimensions={2} | all-to-all | bytes 1048576 | tf_op jit(solution)/shard_map/while/body/eval_jaxpr/all_to_all | solution.py:172
  375.0 6.7 %all-to-all-start.2 = ((f32[2,2,256,128]{3,1,0,2:T(2,128)}), f32[2,2,256,128]{3,1,0,2:T(2,128)S(1)}, u32[]{:S(2)}, u32[]{:S(2)}) async-start(f32[2,2,256,128]{3,1,0,2:T(2,128)} %copy.323), calls=%async_computation.2 | async-start | bytes 1048576 | tf_op jit(solution)/shard_map/while/body/eval_jaxpr/all_to_all | solution.py:181
  381.7 9.4 %all-to-all-done.2 = f32[2,2,256,128]{3,1,0,2:T(2,128)S(1)} async-done(((f32[2,2,256,128]{3,1,0,2:T(2,128)}), f32[2,2,256,128]{3,1,0,2:T(2,128)S(1)}, u32[]{:S(2)}, u32[]{:S(2)}) %all-to-all-start.2) | async-done | bytes 524320 | tf_op jit(solution)/shard_map/while/body/eval_jaxpr/all_to_all | solution.py:181
  392.1 2.7 pad_maximum_fusion.32
  395.6 6.3 %all-to-all-start.3 = ((f32[256,1,4]{2,1,0:T(1,128)}), f32[256,1,4]{2,1,0:T(1,128)S(1)}, u32[]{:S(2)}, u32[]{:S(2)}) async-start(f32[256,1,4]{2,1,0:T(1,128)} %broadcast_in_dim.26), calls=%async_computation.3 | async-start | bytes 262144 | tf_op jit(solution)/shard_map/while/body/eval_jaxpr/all_to_all | solution.py:194
  401.9 13.0 %all-to-all-done.3 = f32[256,1,4]{2,1,0:T(1,128)S(1)} async-done(((f32[256,1,4]{2,1,0:T(1,128)}), f32[256,1,4]{2,1,0:T(1,128)S(1)}, u32[]{:S(2)}, u32[]{:S(2)}) %all-to-all-start.3) | async-done | bytes 4128 | tf_op jit(solution)/shard_map/while/body/eval_jaxpr/all_to_all | solution.py:194
  (218 shorter events, 78.7 us)
Async XLA Ops:
  0.6 130.5 %copy-start = (f32[2,2,64,8,128]{4,3,2,1,0:T(8,128)S(1)}, f32[2,2,64,8,128]{4,3,2,1,0:T(8,128)}, u32[]{:S(2)}) copy-start(f32[2,2,64,8,128]{4,3,2,1,0:T(8,128)} %param.22) | copy-start | bytes 3145732
  1.6 9.4 %collective-permute-start = (bf16[2,2,32,128]{3,2,1,0:T(8,128)(2,1)S(1)}, bf16[2,2,32,128]{3,2,1,0:T(8,128)(2,1)S(1)}, u32[]{:S(2)}, u32[]{:S(2)}) collective-permute-start(bf16[2,2,32,128]{3,2,1,0:T(8,128)(2,1)S(1)} %convert_element_type.146), channel_id=1, source_target_pairs={{0,8},{8,16},{16,24},{24,32},{32,40},{40,48},{48,56},{56,64},{64,7... | collective-permute-start | bytes 98312 | tf_op jit(solution)/shard_map/ppermute | solution.py:26
  5.5 5.5 %collective-permute-start.1 = (bf16[2,2,32,128]{3,2,1,0:T(8,128)(2,1)S(1)}, bf16[2,2,32,128]{3,2,1,0:T(8,128)(2,1)S(1)}, u32[]{:S(2)}, u32[]{:S(2)}) collective-permute-start(bf16[2,2,32,128]{3,2,1,0:T(8,128)(2,1)S(1)} %convert_element_type.146), channel_id=1, source_target_pairs={{8,0},{16,8},{24,16},{32,24},{40,32},{48,40},{56,48},{64,56},{72,6... | collective-permute-start | bytes 98312 | tf_op jit(solution)/shard_map/ppermute | solution.py:28
  11.1 9.0 %collective-permute-start.2 = (bf16[2,6,2,128]{3,2,1,0:T(2,128)(2,1)S(1)}, bf16[2,6,2,128]{3,2,1,0:T(2,128)(2,1)S(1)}, u32[]{:S(2)}, u32[]{:S(2)}) collective-permute-start(bf16[2,6,2,128]{3,2,1,0:T(2,128)(2,1)S(1)} %get-tuple-element.626), channel_id=1, source_target_pairs={{0,1},{1,2},{2,3},{3,4},{4,5},{5,6},{6,7},{8,9},{9,10},{10,11},{11... | collective-permute-start | bytes 18440 | tf_op jit(solution)/shard_map/ppermute | solution.py:26
  15.4 4.9 %collective-permute-start.3 = (bf16[2,6,2,128]{3,2,1,0:T(2,128)(2,1)S(1)}, bf16[2,6,2,128]{3,2,1,0:T(2,128)(2,1)S(1)}, u32[]{:S(2)}, u32[]{:S(2)}) collective-permute-start(bf16[2,6,2,128]{3,2,1,0:T(2,128)(2,1)S(1)} %get-tuple-element.627), channel_id=1, source_target_pairs={{1,0},{2,1},{3,2},{4,3},{5,4},{6,5},{7,6},{9,8},{10,9},{11,10},{12... | collective-permute-start | bytes 18440 | tf_op jit(solution)/shard_map/ppermute | solution.py:28
  24.1 2.5 copy-start.3
  47.2 8.2 %copy-start.13 = (f32[256,1,256]{2,0,1:T(8,128)S(1)}, f32[256,1,256]{2,0,1:T(8,128)}, u32[]{:S(2)}) copy-start(f32[256,1,256]{2,0,1:T(8,128)} %cosine_multiply_fusion) | copy-start | bytes 786436
  47.2 8.2 %copy-start.14 = (f32[256,1,256]{2,0,1:T(8,128)S(1)}, f32[256,1,256]{2,0,1:T(8,128)}, u32[]{:S(2)}) copy-start(f32[256,1,256]{2,0,1:T(8,128)} %fusion.100) | copy-start | bytes 786436
  48.9 13.7 %copy-start.2 = (bf16[32,2,32,128]{3,0,2,1:T(8,128)(2,1)}, bf16[32,2,32,128]{3,0,2,1:T(8,128)(2,1)S(1)}, u32[]{:S(2)}) copy-start(bf16[32,2,32,128]{3,0,2,1:T(8,128)(2,1)S(1)} %add_convert_fusion) | copy-start | bytes 1572868
  48.9 21.3 %copy-start.21 = (bf16[3,3,3,2,32]{4,3,2,1,0:T(2,128)(2,1)S(1)}, bf16[3,3,3,2,32]{4,3,2,1,0:T(2,128)(2,1)}, u32[]{:S(2)}) copy-start(bf16[3,3,3,2,32]{4,3,2,1,0:T(2,128)(2,1)} %param.19) | copy-start | bytes 10372
  49.0 22.0 %copy-start.12 = (f32[2,2,2,256,128]{4,3,2,1,0:T(8,128)S(1)}, f32[2,2,2,256,128]{4,3,2,1,0:T(8,128)}, u32[]{:S(2)}) copy-start(f32[2,2,2,256,128]{4,3,2,1,0:T(8,128)} %param.21) | copy-start | bytes 3145732
  49.0 8.8 %collective-permute-start.4 = (bf16[32,1,32,128]{3,0,2,1:T(8,128)(2,1)S(1)}, bf16[32,1,32,128]{3,0,2,1:T(8,128)(2,1)S(1)}, u32[]{:S(2)}, u32[]{:S(2)}) collective-permute-start(bf16[32,1,32,128]{3,0,2,1:T(8,128)(2,1)S(1)} %get-tuple-element.620), channel_id=1, source_target_pairs={{0,8},{8,16},{16,24},{24,32},{32,40},{40,48},{48,56},{56,64},{64,7... | collective-permute-start | bytes 786440 | tf_op jit(solution)/shard_map/ppermute | solution.py:26
  53.1 8.8 %collective-permute-start.5 = (bf16[32,1,32,128]{3,0,2,1:T(8,128)(2,1)S(1)}, bf16[32,1,32,128]{3,0,2,1:T(8,128)(2,1)S(1)}, u32[]{:S(2)}, u32[]{:S(2)}) collective-permute-start(bf16[32,1,32,128]{3,0,2,1:T(8,128)(2,1)S(1)} %get-tuple-element.621), channel_id=1, source_target_pairs={{8,0},{16,8},{24,16},{32,24},{40,32},{48,40},{56,48},{64,56},{72,6... | collective-permute-start | bytes 786440 | tf_op jit(solution)/shard_map/ppermute | solution.py:28
  61.9 7.5 %copy-start.11 = (bf16[32,1,32,128]{3,0,2,1:T(8,128)(2,1)}, bf16[32,1,32,128]{3,0,2,1:T(8,128)(2,1)S(1)}, u32[]{:S(2)}) copy-start(bf16[32,1,32,128]{3,0,2,1:T(8,128)(2,1)S(1)} %collective-permute-done.5) | copy-start | bytes 786436
  62.6 8.7 %collective-permute-start.6 = (bf16[32,4,1,128]{3,0,2,1:T(8,128)(2,1)}, bf16[32,4,1,128]{3,0,2,1:T(8,128)(2,1)S(1)}, u32[]{:S(2)}, u32[]{:S(2)}) collective-permute-start(bf16[32,4,1,128]{3,0,2,1:T(8,128)(2,1)} %get-tuple-element.612), channel_id=1, source_target_pairs={{0,1},{1,2},{2,3},{3,4},{4,5},{5,6},{6,7},{8,9},{9,10},{10,11},{11... | collective-permute-start | bytes 98312 | tf_op jit(solution)/shard_map/ppermute | solution.py:26
  67.5 5.3 %collective-permute-start.7 = (bf16[32,4,1,128]{3,0,2,1:T(8,128)(2,1)S(1)}, bf16[32,4,1,128]{3,0,2,1:T(8,128)(2,1)}, u32[]{:S(2)}, u32[]{:S(2)}) collective-permute-start(bf16[32,4,1,128]{3,0,2,1:T(8,128)(2,1)S(1)} %get-tuple-element.613), channel_id=1, source_target_pairs={{1,0},{2,1},{3,2},{4,3},{5,4},{6,5},{7,6},{9,8},{10,9},{11,10},{12... | collective-permute-start | bytes 98312 | tf_op jit(solution)/shard_map/ppermute | solution.py:28
  71.4 0.6 copy-start.20
  90.0 0.6 copy-start.10
  104.6 5.0 %copy-start.4 = (f32[1,256,2,256]{3,1,2,0:T(8,128)S(1)}, f32[1,256,2,256]{3,1,2,0:T(8,128)}, u32[]{:S(2)}) copy-start(f32[1,256,2,256]{3,1,2,0:T(8,128)} %get-tuple-element.615) | copy-start | bytes 1572868
  104.6 5.0 %copy-start.5 = (f32[1,256,2,256]{3,1,2,0:T(8,128)S(1)}, f32[1,256,2,256]{3,1,2,0:T(8,128)}, u32[]{:S(2)}) copy-start(f32[1,256,2,256]{3,1,2,0:T(8,128)} %get-tuple-element.622) | copy-start | bytes 1572868
  109.6 21.4 %copy-start.19 = (f32[64,1,64]{2,0,1:T(8,128)S(1)}, f32[64,1,64]{2,0,1:T(8,128)}, u32[]{:S(2)}) copy-start(f32[64,1,64]{2,0,1:T(8,128)} %cosine_multiply_fusion.2) | copy-start | bytes 49156
  113.5 19.3 %copy-start.22 = (s32[64,8]{0,1:T(8,128)S(1)}, s32[64,8]{0,1:T(8,128)}, u32[]{:S(2)}) copy-start(s32[64,8]{0,1:T(8,128)} %param.23) | copy-start | bytes 6148
  113.5 33.3 %all-to-all-start.4 = ((bf16[2,2,2,256,128]{4,1,2,0,3:T(2,128)(2,1)}), bf16[2,2,2,256,128]{4,1,2,0,3:T(2,128)(2,1)}, u32[]{:S(2)}, u32[]{:S(2)}) async-start(bf16[2,2,2,256,128]{4,1,2,0,3:T(2,128)(2,1)} %copy.201), calls=%async_computation.4 | async-start | bytes 1048576 | tf_op jit(solution)/shard_map/all_to_all | solution.py:162
  131.0 17.1 %copy-start.16 = (f32[1,64,2,64]{3,1,2,0:T(8,128)}, f32[1,64,2,64]{3,1,2,0:T(8,128)S(1)}, u32[]{:S(2)}) copy-start(f32[1,64,2,64]{3,1,2,0:T(8,128)S(1)} %get-tuple-element.629) | copy-start | bytes 98308
  131.1 17.1 %copy-start.17 = (f32[1,64,2,64]{3,1,2,0:T(8,128)}, f32[1,64,2,64]{3,1,2,0:T(8,128)S(1)}, u32[]{:S(2)}) copy-start(f32[1,64,2,64]{3,1,2,0:T(8,128)S(1)} %get-tuple-element.634) | copy-start | bytes 98308
  131.1 17.6 %copy-start.15 = (f32[1,64,2,64]{3,1,2,0:T(8,128)}, f32[1,64,2,64]{3,1,2,0:T(8,128)S(1)}, u32[]{:S(2)}) copy-start(f32[1,64,2,64]{3,1,2,0:T(8,128)S(1)} %get-tuple-element.628) | copy-start | bytes 98308
  131.1 17.6 %copy-start.18 = (f32[1,64,2,64]{3,1,2,0:T(8,128)}, f32[1,64,2,64]{3,1,2,0:T(8,128)S(1)}, u32[]{:S(2)}) copy-start(f32[1,64,2,64]{3,1,2,0:T(8,128)S(1)} %get-tuple-element.635) | copy-start | bytes 98308
  146.8 1.4 copy-start.9
  150.2 30.9 %copy-start.6 = (f32[1,256,2,256]{3,1,2,0:T(8,128)S(1)}, f32[1,256,2,256]{3,1,2,0:T(8,128)}, u32[]{:S(2)}) copy-start(f32[1,256,2,256]{3,1,2,0:T(8,128)} %get-tuple-element.614) | copy-start | bytes 1572868
  150.2 30.9 %copy-start.7 = (f32[1,256,2,256]{3,1,2,0:T(8,128)S(1)}, f32[1,256,2,256]{3,1,2,0:T(8,128)}, u32[]{:S(2)}) copy-start(f32[1,256,2,256]{3,1,2,0:T(8,128)} %get-tuple-element.623) | copy-start | bytes 1572868
  186.1 16.7 %all-to-all-start.6 = ((f32[2,2,256,128]{3,1,0,2:T(2,128)}), f32[2,2,256,128]{3,1,0,2:T(2,128)}, u32[]{:S(2)}, u32[]{:S(2)}) async-start(f32[2,2,256,128]{3,1,0,2:T(2,128)} %copy.209), calls=%async_computation.6 | async-start | bytes 1048576 | tf_op jit(solution)/shard_map/all_to_all | solution.py:181
  222.0 22.6 %copy-start.8 = (f32[2,64,2,64]{3,1,2,0:T(8,128)S(1)}, f32[2,64,2,64]{3,1,2,0:T(8,128)}, u32[]{:S(2)}) copy-start(f32[2,64,2,64]{3,1,2,0:T(8,128)} %get-tuple-element.916) | copy-start | bytes 196612 | tf_op jit(solution)/shard_map/while
  244.6 21.6 %copy-start.1 = (f32[2,256,2,256]{3,1,2,0:T(8,128)S(1)}, f32[2,256,2,256]{3,1,2,0:T(8,128)}, u32[]{:S(2)}) copy-start(f32[2,256,2,256]{3,1,2,0:T(8,128)} %get-tuple-element.917) | copy-start | bytes 3145732 | tf_op jit(solution)/shard_map/while
  268.3 16.1 %all-to-all-start.2 = ((f32[2,2,256,128]{3,1,0,2:T(2,128)}), f32[2,2,256,128]{3,1,0,2:T(2,128)S(1)}, u32[]{:S(2)}, u32[]{:S(2)}) async-start(f32[2,2,256,128]{3,1,0,2:T(2,128)} %copy.323), calls=%async_computation.2 | async-start | bytes 1048576 | tf_op jit(solution)/shard_map/while/body/eval_jaxpr/all_to_all | solution.py:181
  288.9 19.3 %all-to-all-start.3 = ((f32[256,1,4]{2,1,0:T(1,128)}), f32[256,1,4]{2,1,0:T(1,128)S(1)}, u32[]{:S(2)}, u32[]{:S(2)}) async-start(f32[256,1,4]{2,1,0:T(1,128)} %broadcast_in_dim.26), calls=%async_computation.3 | async-start | bytes 262144 | tf_op jit(solution)/shard_map/while/body/eval_jaxpr/all_to_all | solution.py:194
  330.4 20.8 %copy-start.8 = (f32[2,64,2,64]{3,1,2,0:T(8,128)S(1)}, f32[2,64,2,64]{3,1,2,0:T(8,128)}, u32[]{:S(2)}) copy-start(f32[2,64,2,64]{3,1,2,0:T(8,128)} %get-tuple-element.916) | copy-start | bytes 196612 | tf_op jit(solution)/shard_map/while
  351.3 21.6 %copy-start.1 = (f32[2,256,2,256]{3,1,2,0:T(8,128)S(1)}, f32[2,256,2,256]{3,1,2,0:T(8,128)}, u32[]{:S(2)}) copy-start(f32[2,256,2,256]{3,1,2,0:T(8,128)} %get-tuple-element.917) | copy-start | bytes 3145732 | tf_op jit(solution)/shard_map/while
  375.0 16.1 %all-to-all-start.2 = ((f32[2,2,256,128]{3,1,0,2:T(2,128)}), f32[2,2,256,128]{3,1,0,2:T(2,128)S(1)}, u32[]{:S(2)}, u32[]{:S(2)}) async-start(f32[2,2,256,128]{3,1,0,2:T(2,128)} %copy.323), calls=%async_computation.2 | async-start | bytes 1048576 | tf_op jit(solution)/shard_map/while/body/eval_jaxpr/all_to_all | solution.py:181
  395.6 19.3 %all-to-all-start.3 = ((f32[256,1,4]{2,1,0:T(1,128)}), f32[256,1,4]{2,1,0:T(1,128)S(1)}, u32[]{:S(2)}, u32[]{:S(2)}) async-start(f32[256,1,4]{2,1,0:T(1,128)} %broadcast_in_dim.26), calls=%async_computation.3 | async-start | bytes 262144 | tf_op jit(solution)/shard_map/while/body/eval_jaxpr/all_to_all | solution.py:194

commit v2 on v0

--- a/solution.py
+++ b/solution.py
@@ -201,7 +201,7 @@
     mixed = (hidden.astype(jnp.float32) + jax.nn.silu(conv_shifted(hidden_wide, w_mid))).astype(
         jnp.bfloat16
     )
-    noise_pred = conv_layer(mixed, w_out)
+    noise_pred = conv_shifted(extended(mixed, (("slab", 1), ("coil", 2)), 1), w_out)
     estimate = (noisy - jnp.sqrt(1.0 - signal_level) * noise_pred) / jnp.sqrt(signal_level)
     depth_full = kdata.shape[2]
     rows_full = sens.shape[3]

time: 394 us -> 399 us (1.013)
  transfers between devices with their start and end apart: 14 -> 14, of which waited for: 10 -> 9; matrix products, arithmetic and copies ran while one was open for 5% -> 6% of each run, Pallas kernels for 0% -> 0%
where the time goes in v2:
time: 399 us; the launch traced here: 397 us
  blocking collectives  155 us (39%)
  starting transfers between devices  73.8 us (18%)
  waiting for transfers between devices  69.4 us (17%)
  other arithmetic  33 us (8%)
  local copies, waits for them, and re-layouts  32 us (8%)
  matrix products  24.2 us (6%)
  loops' own time  7.89 us (2%)
    all_to_all x3, blocking collectives, coil_term(): lax.all_to_all(back.astype(link_type), 'slab', split_axis=2, concat_axis=...  71.4 us
    all_to_all x2, blocking collectives, coil_term(): lax.all_to_all(spectrum.astype(jnp.bfloat16), 'slab', split_axis=3, conca...  42.1 us
    all_gather x3, blocking collectives, gather_rows(): return lax.all_gather(value, 'coil', axis=2, tiled=True)  41 us
    all_to_all x2, waiting for transfers between devices, global_sums(): lax.all_to_all(spread, axes, split_axis=0, concat_axis=0, tiled=True)  26 us
    all_to_all x3, waiting for transfers between devices, combine_coils(): lax.all_to_all(partial_value, 'coil', split_axis=2, concat_axis=0, tiled=...  23.7 us
    all_to_all x3, starting transfers between devices, combine_coils(): lax.all_to_all(partial_value, 'coil', split_axis=2, concat_axis=0, tiled=...  20.6 us
    ppermute x4, starting transfers between devices, extended(): lax.ppermute(tail, axis, [(i, (i + 1) % count) for i in range(ends)])  17.2 us
    all_to_all x1, starting transfers between devices, coil_term(): lax.all_to_all(spectrum.astype(jnp.bfloat16), 'slab', split_axis=3, conca...  16.6 us
  transfers between devices with their start and end apart: 14, of which 9 were waited for; matrix products, arithmetic and copies ran while one was open for 6% of the time, Pallas kernels for 0%

profile of v2, /device:TPU:1, one launch (start us, length us, event | category | flops | bytes accessed | tf_op | source)
XLA Modules:
  0.0 397.1 jit_solution(9396790960382346135)
XLA Ops:
  1.6 3.9 collective-permute-start
  5.5 1.3 collective-permute-start.1
  6.8 1.7 cosine_multiply_fusion
  8.5 1.7 fusion.110
  10.2 1.7 sine_multiply_fusion
  13.7 4.0 %collective-permute-start.2 = (bf16[2,6,2,128]{3,2,1,0:T(2,128)(2,1)S(1)}, bf16[2,6,2,128]{3,2,1,0:T(2,128)(2,1)S(1)}, u32[]{:S(2)}, u32[]{:S(2)}) collective-permute-start(bf16[2,6,2,128]{3,2,1,0:T(2,128)(2,1)S(1)} %get-tuple-element.347), channel_id=1, source_target_pairs={{0,1},{1,2},{2,3},{3,4},{4,5},{5,6},{6,7},{8,9},{9,10},{10,11},{11... | collective-permute-start | bytes 18440 | tf_op jit(solution)/shard_map/ppermute | solution.py:26
  17.7 1.9 collective-permute-start.3
  25.1 1.3 fusion.25
  30.8 4.3 %collective-permute-start.4 = (bf16[32,1,32,128]{3,0,2,1:T(8,128)(2,1)S(1)}, bf16[32,1,32,128]{3,0,2,1:T(8,128)(2,1)S(1)}, u32[]{:S(2)}, u32[]{:S(2)}) collective-permute-start(bf16[32,1,32,128]{3,0,2,1:T(8,128)(2,1)S(1)} %get-tuple-element.332), channel_id=1, source_target_pairs={{0,8},{8,16},{16,24},{24,32},{32,40},{40,48},{48,56},{56,64},{64,7... | collective-permute-start | bytes 786440 | tf_op jit(solution)/shard_map/ppermute | solution.py:26
  37.8 2.0 collective-permute-done.4
  39.8 4.1 %collective-permute-done.5 = bf16[32,1,32,128]{3,0,2,1:T(8,128)(2,1)S(1)} collective-permute-done((bf16[32,1,32,128]{3,0,2,1:T(8,128)(2,1)S(1)}, bf16[32,1,32,128]{3,0,2,1:T(8,128)(2,1)S(1)}, u32[]{:S(2)}, u32[]{:S(2)}) %collective-permute-start.5) | collective-permute-done | bytes 262176 | tf_op jit(solution)/shard_map/ppermute | solution.py:28
  43.9 4.9 %collective-permute-start.6 = (bf16[32,4,1,128]{3,0,2,1:T(8,128)(2,1)S(1)}, bf16[32,4,1,128]{3,0,2,1:T(8,128)(2,1)S(1)}, u32[]{:S(2)}, u32[]{:S(2)}) collective-permute-start(bf16[32,4,1,128]{3,0,2,1:T(8,128)(2,1)S(1)} %get-tuple-element.324), channel_id=1, source_target_pairs={{0,1},{1,2},{2,3},{3,4},{4,5},{5,6},{6,7},{8,9},{9,10},{10,11},{11... | collective-permute-start | bytes 98312 | tf_op jit(solution)/shard_map/ppermute | solution.py:26
  48.9 2.1 collective-permute-start.7
  55.4 1.6 copy.270
  57.0 3.0 select_maximum_fusion
  66.0 13.7 %all_gather.6 = f32[2,2,256,128]{3,0,2,1:T(2,128)S(1)} all-gather(f32[2,2,32,128]{3,0,2,1:T(2,128)S(1)} %get-tuple-element.368), channel_id=1, replica_groups=mesh['slab'=32,'coil'=8] {'coil'}, dimensions={2}, use_global_device_ids=true | all-gather | bytes 589824 | tf_op jit(solution)/shard_map/all_gather | solution.py:180
  82.0 1.8 copy.274
  84.8 1.9 fusion.79
  86.7 2.0 copy.275
  88.7 16.6 %all-to-all-start.4 = ((bf16[2,2,2,256,128]{4,1,2,0,3:T(2,128)(2,1)}), bf16[2,2,2,256,128]{4,1,2,0,3:T(2,128)(2,1)}, u32[]{:S(2)}, u32[]{:S(2)}) async-start(bf16[2,2,2,256,128]{4,1,2,0,3:T(2,128)(2,1)} %copy.275), calls=%async_computation.4 | async-start | bytes 1048576 | tf_op jit(solution)/shard_map/all_to_all | solution.py:155
  107.1 1.7 convolution_bitcast_fusion.8
  108.8 13.2 %all-to-all-done.4 = bf16[2,2,2,256,128]{4,1,2,0,3:T(2,128)(2,1)} async-done(((bf16[2,2,2,256,128]{4,1,2,0,3:T(2,128)(2,1)}), bf16[2,2,2,256,128]{4,1,2,0,3:T(2,128)(2,1)}, u32[]{:S(2)}, u32[]{:S(2)}) %all-to-all-start.4) | async-done | bytes 524320 | tf_op jit(solution)/shard_map/all_to_all | solution.py:155
  125.4 30.8 %all_to_all.110 = f32[2,2,64,8,128]{4,1,3,0,2:T(2,128)S(1)} all-to-all(f32[2,2,64,8,128]{4,1,3,0,2:T(2,128)S(1)} %copy.279), channel_id=1, replica_groups=mesh['slab'=32,'coil'=8] {'slab'}, dimensions={2} | all-to-all | bytes 2097152 | tf_op jit(solution)/shard_map/all_to_all | solution.py:165
  156.3 1.9 convolution_bitcast_fusion.4
  159.2 2.0 copy.283
  161.3 7.2 %all-to-all-start.6 = ((f32[2,2,256,128]{3,1,0,2:T(2,128)}), f32[2,2,256,128]{3,1,0,2:T(2,128)}, u32[]{:S(2)}, u32[]{:S(2)}) async-start(f32[2,2,256,128]{3,1,0,2:T(2,128)} %copy.283), calls=%async_computation.6 | async-start | bytes 1048576 | tf_op jit(solution)/shard_map/all_to_all | solution.py:174
  168.6 1.5 pad_maximum_fusion.11
  170.2 2.8 pad_maximum_fusion.4
  173.0 4.9 %all-to-all-done.6 = f32[2,2,256,128]{3,1,0,2:T(2,128)} async-done(((f32[2,2,256,128]{3,1,0,2:T(2,128)}), f32[2,2,256,128]{3,1,0,2:T(2,128)}, u32[]{:S(2)}, u32[]{:S(2)}) %all-to-all-start.6) | async-done | bytes 524320 | tf_op jit(solution)/shard_map/all_to_all | solution.py:174
  179.8 215.1 %while.21 = (s32[]{:T(128)}, f32[2,2,32,128]{3,1,0,2:T(2,128)S(1)}, f32[2,2,32,128]{3,1,0,2:T(2,128)S(1)}, f32[2,2,32,128]{3,1,0,2:T(2,128)S(1)}, f32[2,2,32,128...) while((s32[]{:T(128)}, f32[2,2,32,128]{3,1,0,2:T(2,128)S(1)}, ...), condition=%wide.region_12.13_spmd.clone, body=%wide.region_3.12_spmd.clone.sunk | while | flops 2016658432 | bytes 33634820 | solution.py:251
  179.8 13.9 %all_gather.9 = f32[2,2,256,128]{3,1,0,2:T(2,128)S(1)} all-gather(f32[2,2,32,128]{3,1,0,2:T(2,128)S(1)} %get-tuple-element.518), channel_id=1, replica_groups=mesh['slab'=32,'coil'=8] {'coil'}, dimensions={2}, use_global_device_ids=true | all-gather | bytes 589824 | tf_op jit(solution)/shard_map/while/body/eval_jaxpr/all_gather | solution.py:180
  194.3 2.2 fusion.243
  197.1 21.9 %all_to_all.111 = bf16[2,2,2,256,128]{4,1,2,0,3:T(2,128)(2,1)S(1)} all-to-all(bf16[2,2,2,256,128]{4,1,2,0,3:T(2,128)(2,1)S(1)} %copy.397), channel_id=1, replica_groups=mesh['slab'=32,'coil'=8] {'slab'}, dimensions={3} | all-to-all | bytes 1048576 | tf_op jit(solution)/shard_map/while/body/eval_jaxpr/all_to_all | solution.py:155
  220.9 20.3 %all_to_all.112 = bf16[2,2,64,8,128]{4,1,3,0,2:T(2,128)(2,1)S(1)} all-to-all(bf16[2,2,64,8,128]{4,1,3,0,2:T(2,128)(2,1)S(1)} %copy.400), channel_id=1, replica_groups=mesh['slab'=32,'coil'=8] {'slab'}, dimensions={2} | all-to-all | bytes 1048576 | tf_op jit(solution)/shard_map/while/body/eval_jaxpr/all_to_all | solution.py:165
  243.4 6.7 %all-to-all-start.2 = ((f32[2,2,256,128]{3,1,0,2:T(2,128)}), f32[2,2,256,128]{3,1,0,2:T(2,128)S(1)}, u32[]{:S(2)}, u32[]{:S(2)}) async-start(f32[2,2,256,128]{3,1,0,2:T(2,128)} %copy.402), calls=%async_computation.2 | async-start | bytes 1048576 | tf_op jit(solution)/shard_map/while/body/eval_jaxpr/all_to_all | solution.py:174
  250.2 9.4 %all-to-all-done.2 = f32[2,2,256,128]{3,1,0,2:T(2,128)S(1)} async-done(((f32[2,2,256,128]{3,1,0,2:T(2,128)}), f32[2,2,256,128]{3,1,0,2:T(2,128)S(1)}, u32[]{:S(2)}, u32[]{:S(2)}) %all-to-all-start.2) | async-done | bytes 524320 | tf_op jit(solution)/shard_map/while/body/eval_jaxpr/all_to_all | solution.py:174
  260.5 2.5 pad_maximum_fusion.32
  263.7 6.3 %all-to-all-start.3 = ((f32[256,1,4]{2,1,0:T(1,128)}), f32[256,1,4]{2,1,0:T(1,128)S(1)}, u32[]{:S(2)}, u32[]{:S(2)}) async-start(f32[256,1,4]{2,1,0:T(1,128)} %broadcast_in_dim.26), calls=%async_computation.3 | async-start | bytes 262144 | tf_op jit(solution)/shard_map/while/body/eval_jaxpr/all_to_all | solution.py:187
  270.0 13.0 %all-to-all-done.3 = f32[256,1,4]{2,1,0:T(1,128)S(1)} async-done(((f32[256,1,4]{2,1,0:T(1,128)}), f32[256,1,4]{2,1,0:T(1,128)S(1)}, u32[]{:S(2)}, u32[]{:S(2)}) %all-to-all-start.3) | async-done | bytes 4128 | tf_op jit(solution)/shard_map/while/body/eval_jaxpr/all_to_all | solution.py:187
  288.5 13.4 %all_gather.9 = f32[2,2,256,128]{3,1,0,2:T(2,128)S(1)} all-gather(f32[2,2,32,128]{3,1,0,2:T(2,128)S(1)} %get-tuple-element.518), channel_id=1, replica_groups=mesh['slab'=32,'coil'=8] {'coil'}, dimensions={2}, use_global_device_ids=true | all-gather | bytes 589824 | tf_op jit(solution)/shard_map/while/body/eval_jaxpr/all_gather | solution.py:180
  302.6 2.2 fusion.243
  305.3 20.2 %all_to_all.111 = bf16[2,2,2,256,128]{4,1,2,0,3:T(2,128)(2,1)S(1)} all-to-all(bf16[2,2,2,256,128]{4,1,2,0,3:T(2,128)(2,1)S(1)} %copy.397), channel_id=1, replica_groups=mesh['slab'=32,'coil'=8] {'slab'}, dimensions={3} | all-to-all | bytes 1048576 | tf_op jit(solution)/shard_map/while/body/eval_jaxpr/all_to_all | solution.py:155
  327.3 20.3 %all_to_all.112 = bf16[2,2,64,8,128]{4,1,3,0,2:T(2,128)(2,1)S(1)} all-to-all(bf16[2,2,64,8,128]{4,1,3,0,2:T(2,128)(2,1)S(1)} %copy.400), channel_id=1, replica_groups=mesh['slab'=32,'coil'=8] {'slab'}, dimensions={2} | all-to-all | bytes 1048576 | tf_op jit(solution)/shard_map/while/body/eval_jaxpr/all_to_all | solution.py:165
  349.9 6.7 %all-to-all-start.2 = ((f32[2,2,256,128]{3,1,0,2:T(2,128)}), f32[2,2,256,128]{3,1,0,2:T(2,128)S(1)}, u32[]{:S(2)}, u32[]{:S(2)}) async-start(f32[2,2,256,128]{3,1,0,2:T(2,128)} %copy.402), calls=%async_computation.2 | async-start | bytes 1048576 | tf_op jit(solution)/shard_map/while/body/eval_jaxpr/all_to_all | solution.py:174
  356.6 9.4 %all-to-all-done.2 = f32[2,2,256,128]{3,1,0,2:T(2,128)S(1)} async-done(((f32[2,2,256,128]{3,1,0,2:T(2,128)}), f32[2,2,256,128]{3,1,0,2:T(2,128)S(1)}, u32[]{:S(2)}, u32[]{:S(2)}) %all-to-all-start.2) | async-done | bytes 524320 | tf_op jit(solution)/shard_map/while/body/eval_jaxpr/all_to_all | solution.py:174
  366.9 2.5 pad_maximum_fusion.32
  370.1 6.3 %all-to-all-start.3 = ((f32[256,1,4]{2,1,0:T(1,128)}), f32[256,1,4]{2,1,0:T(1,128)S(1)}, u32[]{:S(2)}, u32[]{:S(2)}) async-start(f32[256,1,4]{2,1,0:T(1,128)} %broadcast_in_dim.26), calls=%async_computation.3 | async-start | bytes 262144 | tf_op jit(solution)/shard_map/while/body/eval_jaxpr/all_to_all | solution.py:187
  376.5 13.0 %all-to-all-done.3 = f32[256,1,4]{2,1,0:T(1,128)S(1)} async-done(((f32[256,1,4]{2,1,0:T(1,128)}), f32[256,1,4]{2,1,0:T(1,128)S(1)}, u32[]{:S(2)}, u32[]{:S(2)}) %all-to-all-start.3) | async-done | bytes 4128 | tf_op jit(solution)/shard_map/while/body/eval_jaxpr/all_to_all | solution.py:187
  (228 shorter events, 54.9 us)
Async XLA Ops:
  0.6 106.5 %copy-start = (f32[2,2,64,8,128]{4,3,2,1,0:T(8,128)S(1)}, f32[2,2,64,8,128]{4,3,2,1,0:T(8,128)}, u32[]{:S(2)}) copy-start(f32[2,2,64,8,128]{4,3,2,1,0:T(8,128)} %param.18) | copy-start | bytes 3145732
  1.6 12.0 %collective-permute-start = (bf16[2,2,32,128]{3,2,1,0:T(8,128)(2,1)S(1)}, bf16[2,2,32,128]{3,2,1,0:T(8,128)(2,1)S(1)}, u32[]{:S(2)}, u32[]{:S(2)}) collective-permute-start(bf16[2,2,32,128]{3,2,1,0:T(8,128)(2,1)S(1)} %convert_element_type.137), channel_id=1, source_target_pairs={{0,8},{8,16},{16,24},{24,32},{32,40},{40,48},{48,56},{56,64},{64,7... | collective-permute-start | bytes 98312 | tf_op jit(solution)/shard_map/ppermute | solution.py:26
  5.5 8.1 %collective-permute-start.1 = (bf16[2,2,32,128]{3,2,1,0:T(8,128)(2,1)S(1)}, bf16[2,2,32,128]{3,2,1,0:T(8,128)(2,1)S(1)}, u32[]{:S(2)}, u32[]{:S(2)}) collective-permute-start(bf16[2,2,32,128]{3,2,1,0:T(8,128)(2,1)S(1)} %convert_element_type.137), channel_id=1, source_target_pairs={{8,0},{16,8},{24,16},{32,24},{40,32},{48,40},{56,48},{64,56},{72,6... | collective-permute-start | bytes 98312 | tf_op jit(solution)/shard_map/ppermute | solution.py:28
  13.7 8.7 %collective-permute-start.2 = (bf16[2,6,2,128]{3,2,1,0:T(2,128)(2,1)S(1)}, bf16[2,6,2,128]{3,2,1,0:T(2,128)(2,1)S(1)}, u32[]{:S(2)}, u32[]{:S(2)}) collective-permute-start(bf16[2,6,2,128]{3,2,1,0:T(2,128)(2,1)S(1)} %get-tuple-element.347), channel_id=1, source_target_pairs={{0,1},{1,2},{2,3},{3,4},{4,5},{5,6},{6,7},{8,9},{9,10},{10,11},{11... | collective-permute-start | bytes 18440 | tf_op jit(solution)/shard_map/ppermute | solution.py:26
  17.7 4.9 %collective-permute-start.3 = (bf16[2,6,2,128]{3,2,1,0:T(2,128)(2,1)S(1)}, bf16[2,6,2,128]{3,2,1,0:T(2,128)(2,1)S(1)}, u32[]{:S(2)}, u32[]{:S(2)}) collective-permute-start(bf16[2,6,2,128]{3,2,1,0:T(2,128)(2,1)S(1)} %get-tuple-element.348), channel_id=1, source_target_pairs={{1,0},{2,1},{3,2},{4,3},{5,4},{6,5},{7,6},{9,8},{10,9},{11,10},{12... | collective-permute-start | bytes 18440 | tf_op jit(solution)/shard_map/ppermute | solution.py:28
  30.2 6.2 %copy-start.9 = (f32[256,1,256]{2,0,1:T(8,128)S(1)}, f32[256,1,256]{2,0,1:T(8,128)}, u32[]{:S(2)}) copy-start(f32[256,1,256]{2,0,1:T(8,128)} %cosine_multiply_fusion) | copy-start | bytes 786436
  30.3 6.2 %copy-start.10 = (f32[256,1,256]{2,0,1:T(8,128)S(1)}, f32[256,1,256]{2,0,1:T(8,128)}, u32[]{:S(2)}) copy-start(f32[256,1,256]{2,0,1:T(8,128)} %fusion.110) | copy-start | bytes 786436
  30.3 6.2 %copy-start.11 = (f32[256,1,256]{2,0,1:T(8,128)S(1)}, f32[256,1,256]{2,0,1:T(8,128)}, u32[]{:S(2)}) copy-start(f32[256,1,256]{2,0,1:T(8,128)} %sine_multiply_fusion) | copy-start | bytes 786436
  30.8 7.0 %copy-start.17 = (bf16[3,3,3,2,32]{4,3,2,1,0:T(2,128)(2,1)S(1)}, bf16[3,3,3,2,32]{4,3,2,1,0:T(2,128)(2,1)}, u32[]{:S(2)}) copy-start(bf16[3,3,3,2,32]{4,3,2,1,0:T(2,128)(2,1)} %param.15) | copy-start | bytes 10372
  30.8 9.0 %collective-permute-start.4 = (bf16[32,1,32,128]{3,0,2,1:T(8,128)(2,1)S(1)}, bf16[32,1,32,128]{3,0,2,1:T(8,128)(2,1)S(1)}, u32[]{:S(2)}, u32[]{:S(2)}) collective-permute-start(bf16[32,1,32,128]{3,0,2,1:T(8,128)(2,1)S(1)} %get-tuple-element.332), channel_id=1, source_target_pairs={{0,8},{8,16},{16,24},{24,32},{32,40},{40,48},{48,56},{56,64},{64,7... | collective-permute-start | bytes 786440 | tf_op jit(solution)/shard_map/ppermute | solution.py:26
  35.1 8.8 %collective-permute-start.5 = (bf16[32,1,32,128]{3,0,2,1:T(8,128)(2,1)S(1)}, bf16[32,1,32,128]{3,0,2,1:T(8,128)(2,1)S(1)}, u32[]{:S(2)}, u32[]{:S(2)}) collective-permute-start(bf16[32,1,32,128]{3,0,2,1:T(8,128)(2,1)S(1)} %get-tuple-element.333), channel_id=1, source_target_pairs={{8,0},{16,8},{24,16},{32,24},{40,32},{48,40},{56,48},{64,56},{72,6... | collective-permute-start | bytes 786440 | tf_op jit(solution)/shard_map/ppermute | solution.py:28
  43.9 11.4 %copy-start.7 = (bf16[32,1,32,128]{3,0,2,1:T(8,128)(2,1)}, bf16[32,1,32,128]{3,0,2,1:T(8,128)(2,1)S(1)}, u32[]{:S(2)}) copy-start(bf16[32,1,32,128]{3,0,2,1:T(8,128)(2,1)S(1)} %collective-permute-done.5) | copy-start | bytes 786436
  43.9 13.0 %collective-permute-start.6 = (bf16[32,4,1,128]{3,0,2,1:T(8,128)(2,1)S(1)}, bf16[32,4,1,128]{3,0,2,1:T(8,128)(2,1)S(1)}, u32[]{:S(2)}, u32[]{:S(2)}) collective-permute-start(bf16[32,4,1,128]{3,0,2,1:T(8,128)(2,1)S(1)} %get-tuple-element.324), channel_id=1, source_target_pairs={{0,1},{1,2},{2,3},{3,4},{4,5},{5,6},{6,7},{8,9},{9,10},{10,11},{11... | collective-permute-start | bytes 98312 | tf_op jit(solution)/shard_map/ppermute | solution.py:26
  48.9 8.1 %collective-permute-start.7 = (bf16[32,4,1,128]{3,0,2,1:T(8,128)(2,1)S(1)}, bf16[32,4,1,128]{3,0,2,1:T(8,128)(2,1)S(1)}, u32[]{:S(2)}, u32[]{:S(2)}) collective-permute-start(bf16[32,4,1,128]{3,0,2,1:T(8,128)(2,1)S(1)} %get-tuple-element.325), channel_id=1, source_target_pairs={{1,0},{2,1},{3,2},{4,3},{5,4},{6,5},{7,6},{9,8},{10,9},{11,10},{12... | collective-permute-start | bytes 98312 | tf_op jit(solution)/shard_map/ppermute | solution.py:28
  60.0 1.0 copy-start.8
  62.1 1.0 copy-start.19
  62.4 1.0 copy-start.20
  62.7 1.0 copy-start.21
  63.1 1.0 copy-start.22
  63.4 1.0 copy-start.16
  63.4 1.0 copy-start.23
  65.3 0.6 copy-start.14
  79.7 5.2 %copy-start.2 = (f32[1,256,2,256]{3,1,2,0:T(8,128)S(1)}, f32[1,256,2,256]{3,1,2,0:T(8,128)}, u32[]{:S(2)}) copy-start(f32[1,256,2,256]{3,1,2,0:T(8,128)} %get-tuple-element.334) | copy-start | bytes 1572868
  88.7 20.1 %copy-start.18 = (s32[64,8]{0,1:T(8,128)S(1)}, s32[64,8]{0,1:T(8,128)}, u32[]{:S(2)}) copy-start(s32[64,8]{0,1:T(8,128)} %param.19) | copy-start | bytes 6148
  88.7 33.3 %all-to-all-start.4 = ((bf16[2,2,2,256,128]{4,1,2,0,3:T(2,128)(2,1)}), bf16[2,2,2,256,128]{4,1,2,0,3:T(2,128)(2,1)}, u32[]{:S(2)}, u32[]{:S(2)}) async-start(bf16[2,2,2,256,128]{4,1,2,0,3:T(2,128)(2,1)} %copy.275), calls=%async_computation.4 | async-start | bytes 1048576 | tf_op jit(solution)/shard_map/all_to_all | solution.py:155
  107.1 16.2 %copy-start.12 = (f32[1,64,2,64]{3,1,2,0:T(8,128)}, f32[1,64,2,64]{3,1,2,0:T(8,128)S(1)}, u32[]{:S(2)}) copy-start(f32[1,64,2,64]{3,1,2,0:T(8,128)S(1)} %get-tuple-element.355) | copy-start | bytes 98308
  107.1 16.8 %copy-start.13 = (f32[1,64,2,64]{3,1,2,0:T(8,128)}, f32[1,64,2,64]{3,1,2,0:T(8,128)S(1)}, u32[]{:S(2)}) copy-start(f32[1,64,2,64]{3,1,2,0:T(8,128)S(1)} %get-tuple-element.356) | copy-start | bytes 98308
  122.0 1.4 copy-start.6
  125.4 30.9 %copy-start.3 = (f32[1,256,2,256]{3,1,2,0:T(8,128)S(1)}, f32[1,256,2,256]{3,1,2,0:T(8,128)}, u32[]{:S(2)}) copy-start(f32[1,256,2,256]{3,1,2,0:T(8,128)} %get-tuple-element.326) | copy-start | bytes 1572868
  125.4 30.9 %copy-start.4 = (f32[1,256,2,256]{3,1,2,0:T(8,128)S(1)}, f32[1,256,2,256]{3,1,2,0:T(8,128)}, u32[]{:S(2)}) copy-start(f32[1,256,2,256]{3,1,2,0:T(8,128)} %get-tuple-element.335) | copy-start | bytes 1572868
  161.3 16.7 %all-to-all-start.6 = ((f32[2,2,256,128]{3,1,0,2:T(2,128)}), f32[2,2,256,128]{3,1,0,2:T(2,128)}, u32[]{:S(2)}, u32[]{:S(2)}) async-start(f32[2,2,256,128]{3,1,0,2:T(2,128)} %copy.283), calls=%async_computation.6 | async-start | bytes 1048576 | tf_op jit(solution)/shard_map/all_to_all | solution.py:174
  170.2 2.8 copy-start.15
  197.1 22.6 %copy-start.5 = (f32[2,64,2,64]{3,1,2,0:T(8,128)S(1)}, f32[2,64,2,64]{3,1,2,0:T(8,128)}, u32[]{:S(2)}) copy-start(f32[2,64,2,64]{3,1,2,0:T(8,128)} %get-tuple-element.544) | copy-start | bytes 196612 | tf_op jit(solution)/shard_map/while
  219.7 21.6 %copy-start.1 = (f32[2,256,2,256]{3,1,2,0:T(8,128)S(1)}, f32[2,256,2,256]{3,1,2,0:T(8,128)}, u32[]{:S(2)}) copy-start(f32[2,256,2,256]{3,1,2,0:T(8,128)} %get-tuple-element.545) | copy-start | bytes 3145732 | tf_op jit(solution)/shard_map/while
  243.4 16.1 %all-to-all-start.2 = ((f32[2,2,256,128]{3,1,0,2:T(2,128)}), f32[2,2,256,128]{3,1,0,2:T(2,128)S(1)}, u32[]{:S(2)}, u32[]{:S(2)}) async-start(f32[2,2,256,128]{3,1,0,2:T(2,128)} %copy.402), calls=%async_computation.2 | async-start | bytes 1048576 | tf_op jit(solution)/shard_map/while/body/eval_jaxpr/all_to_all | solution.py:174
  263.7 19.3 %all-to-all-start.3 = ((f32[256,1,4]{2,1,0:T(1,128)}), f32[256,1,4]{2,1,0:T(1,128)S(1)}, u32[]{:S(2)}, u32[]{:S(2)}) async-start(f32[256,1,4]{2,1,0:T(1,128)} %broadcast_in_dim.26), calls=%async_computation.3 | async-start | bytes 262144 | tf_op jit(solution)/shard_map/while/body/eval_jaxpr/all_to_all | solution.py:187
  305.3 20.8 %copy-start.5 = (f32[2,64,2,64]{3,1,2,0:T(8,128)S(1)}, f32[2,64,2,64]{3,1,2,0:T(8,128)}, u32[]{:S(2)}) copy-start(f32[2,64,2,64]{3,1,2,0:T(8,128)} %get-tuple-element.544) | copy-start | bytes 196612 | tf_op jit(solution)/shard_map/while
  326.2 21.6 %copy-start.1 = (f32[2,256,2,256]{3,1,2,0:T(8,128)S(1)}, f32[2,256,2,256]{3,1,2,0:T(8,128)}, u32[]{:S(2)}) copy-start(f32[2,256,2,256]{3,1,2,0:T(8,128)} %get-tuple-element.545) | copy-start | bytes 3145732 | tf_op jit(solution)/shard_map/while
  349.9 16.1 %all-to-all-start.2 = ((f32[2,2,256,128]{3,1,0,2:T(2,128)}), f32[2,2,256,128]{3,1,0,2:T(2,128)S(1)}, u32[]{:S(2)}, u32[]{:S(2)}) async-start(f32[2,2,256,128]{3,1,0,2:T(2,128)} %copy.402), calls=%async_computation.2 | async-start | bytes 1048576 | tf_op jit(solution)/shard_map/while/body/eval_jaxpr/all_to_all | solution.py:174
  370.1 19.3 %all-to-all-start.3 = ((f32[256,1,4]{2,1,0:T(1,128)}), f32[256,1,4]{2,1,0:T(1,128)S(1)}, u32[]{:S(2)}, u32[]{:S(2)}) async-start(f32[256,1,4]{2,1,0:T(1,128)} %broadcast_in_dim.26), calls=%async_computation.3 | async-start | bytes 262144 | tf_op jit(solution)/shard_map/while/body/eval_jaxpr/all_to_all | solution.py:187
